TPU v7x, 512 devices: a whole 4x4x16 slice. The times are simulated.
512 devices in a mesh: node: 8 (over y, x_lo), space: 64 (over z, x_hi, core).
Axes of the slice: x: 4 (x_hi: 2, x_lo: 2; x = x_hi * 2 + x_lo), y: 4, z: 16, core: 2. Of those that a mesh axis runs over, the one named last changes fastest.
Arguments:
- grain_ids: int32 [256, 16, 128], P('space'), may hold values from 0 to 7
- peak_heat: float32 [256, 16, 128], P('space'), may hold values from 0.5 to 1
Outputs:
- node_states: float32 [8, 8, 256, 16, 128], P('node', None, 'space')
All inputs are finite; a program needn't handle non-finite values.
Results may differ from a plain program's by a relative error of at most 0.0001.
Values sent between devices are 32-bit elements; how exact they have to be, the bound alone decides.
No kernel may reach another device: no remote copies, remote signals or barrier semaphores. Data moves between devices by JAX's collectives and lax.ppermute only.
A program may use at most 64 MiB of HBM per device.

v0:
```python
import math

import jax
import jax.numpy as jnp
import numpy as np
from jax import lax
from jax.sharding import PartitionSpec as P

P_SIZE = 8
NODE_DEV = 1
SWEEPS = 3
JACOBI = 2
STEPS = 2


time_step = 0.25
cross_coef = 1.5
base_heat = 0.45
activation = 3.0


def with_halo(block, sides, width):
    for axis, dim in sides:
        count = lax.axis_size(axis)
        forward = [(i, i + 1) for i in range(count - 1)]
        forward.append((count - 1, 0))
        backward = [(target, source) for source, target in forward]
        low = lax.ppermute(
            lax.slice_in_dim(block, block.shape[dim] - width, None, axis=dim), axis, forward
        )
        high = lax.ppermute(lax.slice_in_dim(block, 0, width, axis=dim), axis, backward)
        block = jnp.concatenate([low, block, high], axis=dim)
    return block


def broadcast(block, axis, source):
    block = jnp.where(lax.axis_index(axis) == source, block, jnp.zeros_like(block))
    return lax.psum(block, axis)


def legendre_pair(count, point):
    before = 1.0
    current = point
    for degree in range(2, count + 1):
        following = ((2 * degree - 1) * point * current - (degree - 1) * before) / degree
        before = current
        current = following
    return (current, before)


def radau_value(count, point):
    high, low = legendre_pair(count, point)
    high_prev, low_prev = legendre_pair(count - 1, point)
    value = high - low
    slope_high = count * (point * high - low) / (point * point - 1.0)
    slope_low = (count - 1) * (point * high_prev - low_prev) / (point * point - 1.0)
    return (value, slope_high - slope_low)


def radau_table(count):
    roots = [1.0]
    for index in range(1, count):
        point = math.cos(2.0 * math.pi * index / (2 * count - 1))
        for repeat in range(100):
            value, slope = radau_value(count, point)
            point = point - value / slope
        roots.append(point)
    roots = sorted(roots)
    times_list = [(value + 1.0) / 2.0 for value in roots]
    times_list[-1] = 1.0
    table = []
    for row_index in range(count):
        upper = times_list[row_index]
        row_values = []
        for column in range(count):
            poly = [1.0]
            for other in range(count):
                if other != column:
                    scale = times_list[column] - times_list[other]
                    shifted = [0.0] + poly
                    scaled = [c * times_list[other] for c in poly] + [0.0]
                    poly = [(shifted[i] - scaled[i]) / scale for i in range(len(shifted))]
            integral_value = 0.0
            for power in range(len(poly)):
                integral_value += poly[power] * upper ** (power + 1) / (power + 1)
            row_values.append(integral_value)
        table.append(row_values)
    return (np.array(times_list), np.array(table))


def drive(field):
    squares = field * field
    total = jnp.sum(squares, axis=-4, keepdims=True)
    return -field + squares * field + 2.0 * cross_coef * field * (total - squares)


def near_sum(extended):
    inner = extended[..., 1:-1, :, :]
    result = extended[..., 2:, :, :] + extended[..., :-2, :, :]
    result = result + jnp.roll(inner, -1, -2) + jnp.roll(inner, 1, -2)
    return result + jnp.roll(inner, -1, -1) + jnp.roll(inner, 1, -1)


def heat_mobility(peak, moment):
    middle = 0.5 * time_step * STEPS
    theta = base_heat + (peak - base_heat) * jnp.exp(-(((moment - middle) / middle) ** 2))
    return jnp.exp(activation * (1.0 - 1.0 / theta))


def rate_on(extended, mobility):
    inner = extended[..., 1:-1, :, :]
    return -mobility * (drive(inner) - (near_sum(extended) - 6.0 * inner))


def relax_on(extended, goal, factor):
    inner = extended[..., 1:-1, :, :]
    return (goal + factor * (near_sum(extended) - drive(inner))) / (1.0 + 6.0 * factor)


def on_device(grain_ids, peak_heat):
    total_nodes = lax.axis_size("node") * NODE_DEV
    node_times, table = radau_table(total_nodes)
    weights = jnp.asarray(table, jnp.float32)
    first = lax.axis_index("node") * NODE_DEV
    times = lax.dynamic_slice_in_dim(jnp.asarray(node_times, jnp.float32), first, NODE_DEV, 0)
    my_rows = lax.dynamic_slice_in_dim(weights, first, NODE_DEV, 0)
    taus = times.reshape((NODE_DEV, 1, 1, 1, 1))
    orders = jnp.arange(P_SIZE, dtype=jnp.int32)
    start = (grain_ids[None] == orders[:, None, None, None]).astype(jnp.float32)
    states = None
    for step_index in range(STEPS):
        moments = (step_index + times) * time_step
        mobility = heat_mobility(peak_heat[None], moments[:, None, None, None])[:, None]
        factor = time_step * taus * mobility
        start_wide = with_halo(start, (("space", 1),), 1)
        rates = rate_on(start_wide[None], mobility)
        states = jnp.broadcast_to(start[None], rates.shape)
        for sweep_index in range(SWEEPS):
            piece = lax.all_gather(rates, "node", axis=0, tiled=True)
            coefs = lax.slice_in_dim(my_rows, 0, piece.shape[0], axis=1)
            quad = jnp.zeros_like(rates) + jnp.tensordot(
                coefs, piece, axes=1, precision=lax.Precision.HIGHEST
            )
            goal = start[None] + time_step * quad - time_step * taus * rates
            last = sweep_index + 1 == SWEEPS
            passes = JACOBI if last else JACOBI + 1
            for relax_index in range(passes):
                extended = with_halo(states, (("space", 2),), 1)
                if relax_index < JACOBI:
                    states = relax_on(extended, goal, factor)
                else:
                    rates = rate_on(extended, mobility)
        if step_index + 1 < STEPS:
            start = broadcast(states[-1], "node", lax.axis_size("node") - 1)
    return states


def solution(mesh):
    in_specs = (P("space", None, None), P("space", None, None))
    out_specs = P("node", None, "space", None, None)
    return jax.shard_map(
        on_device, mesh=mesh, in_specs=in_specs, out_specs=out_specs, check_vma=False
    )
```

profile of v0, /device:TPU:24, one launch (start us, length us, event | category | flops | bytes accessed | tf_op | source)
XLA Modules:
  0.0 647.5 jit_solution(4075357415516616793)
XLA Ops:
  9.3 13.3 %collective-permute-start.1 = (f32[8,1,16,128]{3,2,1,0:T(8,128)S(1)}, f32[8,1,16,128]{3,2,1,0:T(8,128)S(1)}, u32[]{:S(2)}, u32[]{:S(2)}) collective-permute-start(f32[8,1,16,128]{3,2,1,0:T(8,128)S(1)} %get-tuple-element.166), channel_id=1, source_target_pairs={{1,0},{2,1},{3,2},{4,3},{5,4},{6,5},{7,6},{8,7},{9,8},{10,9},{11,1... | collective-permute-start | bytes 196616 | tf_op jit(solution)/shard_map/ppermute | solution.py:31
  27.6 5.7 collective-permute-start.2
  35.7 47.5 %all-gather.7.cloned.1.call-done = f32[8,8,4,16,128]{4,3,2,1,0:T(8,128)} async-done(((f32[1,8,4,16,128]{4,3,2,1,0:T(8,128)}), f32[8,8,4,16,128]{4,3,2,1,0:T(8,128)}) %all-gather.7.cloned.1.call-update) | async-done | bytes 2097168 | tf_op jit(solution)/shard_map/all_gather | solution.py:139
  83.2 4.4 fusion.10
  88.4 7.5 %collective-permute-start.4 = (f32[1,8,1,16,128]{4,3,2,1,0:T(8,128)S(1)}, f32[1,8,1,16,128]{4,3,2,1,0:T(8,128)S(1)}, u32[]{:S(2)}, u32[]{:S(2)}) collective-permute-start(f32[1,8,1,16,128]{4,3,2,1,0:T(8,128)S(1)} %get-tuple-element.155), channel_id=1, source_target_pairs={{1,0},{2,1},{3,2},{4,3},{5,4},{6,5},{7,6},{8,7},{9,8},{10,9},{11,1... | collective-permute-start | bytes 196616 | tf_op jit(solution)/shard_map/ppermute | solution.py:31
  97.9 7.2 %collective-permute-done.5 = f32[1,8,1,16,128]{4,3,2,1,0:T(8,128)S(1)} collective-permute-done((f32[1,8,1,16,128]{4,3,2,1,0:T(8,128)S(1)}, f32[1,8,1,16,128]{4,3,2,1,0:T(8,128)S(1)}, u32[]{:S(2)}, u32[]{:S(2)}) %collective-permute-start.5) | collective-permute-done | bytes 65568 | tf_op jit(solution)/shard_map/ppermute | solution.py:28
  110.2 6.7 %collective-permute-done.7 = f32[1,8,1,16,128]{4,3,2,1,0:T(8,128)S(1)} collective-permute-done((f32[1,8,1,16,128]{4,3,2,1,0:T(8,128)S(1)}, f32[1,8,1,16,128]{4,3,2,1,0:T(8,128)S(1)}, u32[]{:S(2)}, u32[]{:S(2)}) %collective-permute-start.7) | collective-permute-done | bytes 65568 | tf_op jit(solution)/shard_map/ppermute | solution.py:28
  118.1 53.8 %all-gather.9.cloned.1.call-done = f32[8,8,4,16,128]{4,3,2,1,0:T(8,128)} async-done(((f32[1,8,4,16,128]{4,3,2,1,0:T(8,128)}), f32[8,8,4,16,128]{4,3,2,1,0:T(8,128)}) %all-gather.9.cloned.1.call-update) | async-done | bytes 2097168 | tf_op jit(solution)/shard_map/all_gather | solution.py:139
  171.9 4.4 fusion.8
  176.9 7.5 %collective-permute-start.8 = (f32[1,8,1,16,128]{4,3,2,1,0:T(8,128)S(1)}, f32[1,8,1,16,128]{4,3,2,1,0:T(8,128)S(1)}, u32[]{:S(2)}, u32[]{:S(2)}) collective-permute-start(f32[1,8,1,16,128]{4,3,2,1,0:T(8,128)S(1)} %get-tuple-element.135), channel_id=1, source_target_pairs={{1,0},{2,1},{3,2},{4,3},{5,4},{6,5},{7,6},{8,7},{9,8},{10,9},{11,1... | collective-permute-start | bytes 196616 | tf_op jit(solution)/shard_map/ppermute | solution.py:31
  186.4 7.2 %collective-permute-done.9 = f32[1,8,1,16,128]{4,3,2,1,0:T(8,128)S(1)} collective-permute-done((f32[1,8,1,16,128]{4,3,2,1,0:T(8,128)S(1)}, f32[1,8,1,16,128]{4,3,2,1,0:T(8,128)S(1)}, u32[]{:S(2)}, u32[]{:S(2)}) %collective-permute-start.9) | collective-permute-done | bytes 65568 | tf_op jit(solution)/shard_map/ppermute | solution.py:28
  198.7 6.7 %collective-permute-done.11 = f32[1,8,1,16,128]{4,3,2,1,0:T(8,128)S(1)} collective-permute-done((f32[1,8,1,16,128]{4,3,2,1,0:T(8,128)S(1)}, f32[1,8,1,16,128]{4,3,2,1,0:T(8,128)S(1)}, u32[]{:S(2)}, u32[]{:S(2)}) %collective-permute-start.11) | collective-permute-done | bytes 65568 | tf_op jit(solution)/shard_map/ppermute | solution.py:28
  206.7 53.6 %all-gather.11.cloned.1.call-done = f32[8,8,4,16,128]{4,3,2,1,0:T(8,128)} async-done(((f32[1,8,4,16,128]{4,3,2,1,0:T(8,128)}), f32[8,8,4,16,128]{4,3,2,1,0:T(8,128)}) %all-gather.11.cloned.1.call-update) | async-done | bytes 2097168 | tf_op jit(solution)/shard_map/all_gather | solution.py:139
  260.4 4.4 fusion.6
  265.3 7.5 %collective-permute-start.12 = (f32[1,8,1,16,128]{4,3,2,1,0:T(8,128)S(1)}, f32[1,8,1,16,128]{4,3,2,1,0:T(8,128)S(1)}, u32[]{:S(2)}, u32[]{:S(2)}) collective-permute-start(f32[1,8,1,16,128]{4,3,2,1,0:T(8,128)S(1)} %get-tuple-element.115), channel_id=1, source_target_pairs={{1,0},{2,1},{3,2},{4,3},{5,4},{6,5},{7,6},{8,7},{9,8},{10,9},{11,1... | collective-permute-start | bytes 196616 | tf_op jit(solution)/shard_map/ppermute | solution.py:31
  274.8 7.2 %collective-permute-done.13 = f32[1,8,1,16,128]{4,3,2,1,0:T(8,128)S(1)} collective-permute-done((f32[1,8,1,16,128]{4,3,2,1,0:T(8,128)S(1)}, f32[1,8,1,16,128]{4,3,2,1,0:T(8,128)S(1)}, u32[]{:S(2)}, u32[]{:S(2)}) %collective-permute-start.13) | collective-permute-done | bytes 65568 | tf_op jit(solution)/shard_map/ppermute | solution.py:28
  283.2 83.6 %all-reduce.2.cloned.1.call-done = f32[8,4,16,128]{3,2,1,0:T(8,128)} async-done(((f32[8,4,16,128]{3,2,1,0:T(8,128)}), f32[8,4,16,128]{3,2,1,0:T(8,128)}) %all-reduce.2.cloned.1.call-update) | async-done | bytes 262160 | tf_op jit(solution)/shard_map/psum | solution.py:38
  369.6 7.3 %collective-permute-start.15 = (f32[8,1,16,128]{3,2,1,0:T(8,128)S(1)}, f32[8,1,16,128]{3,2,1,0:T(8,128)S(1)}, u32[]{:S(2)}, u32[]{:S(2)}) collective-permute-start(f32[8,1,16,128]{3,2,1,0:T(8,128)S(1)} %get-tuple-element.104), channel_id=1, source_target_pairs={{1,0},{2,1},{3,2},{4,3},{5,4},{6,5},{7,6},{8,7},{9,8},{10,9},{11,1... | collective-permute-start | bytes 196616 | tf_op jit(solution)/shard_map/ppermute | solution.py:31
  381.3 7.3 %collective-permute-start.16 = (f32[1,8,1,16,128]{4,3,2,1,0:T(8,128)S(1)}, f32[1,8,1,16,128]{4,3,2,1,0:T(8,128)S(1)}, u32[]{:S(2)}, u32[]{:S(2)}) collective-permute-start(f32[1,8,1,16,128]{4,3,2,1,0:T(8,128)S(1)} %get-tuple-element.105), channel_id=1, source_target_pairs={{1,0},{2,1},{3,2},{4,3},{5,4},{6,5},{7,6},{8,7},{9,8},{10,9},{11,1... | collective-permute-start | bytes 196616 | tf_op jit(solution)/shard_map/ppermute | solution.py:31
  390.9 49.9 %all-gather.13.cloned.1.call-done = f32[8,8,4,16,128]{4,3,2,1,0:T(8,128)} async-done(((f32[1,8,4,16,128]{4,3,2,1,0:T(8,128)}), f32[8,8,4,16,128]{4,3,2,1,0:T(8,128)}) %all-gather.13.cloned.1.call-update) | async-done | bytes 2097168 | tf_op jit(solution)/shard_map/all_gather | solution.py:139
  446.0 7.5 %collective-permute-start.18 = (f32[1,8,1,16,128]{4,3,2,1,0:T(8,128)S(1)}, f32[1,8,1,16,128]{4,3,2,1,0:T(8,128)S(1)}, u32[]{:S(2)}, u32[]{:S(2)}) collective-permute-start(f32[1,8,1,16,128]{4,3,2,1,0:T(8,128)S(1)} %get-tuple-element.93), channel_id=1, source_target_pairs={{1,0},{2,1},{3,2},{4,3},{5,4},{6,5},{7,6},{8,7},{9,8},{10,9},{11,1... | collective-permute-start | bytes 196616 | tf_op jit(solution)/shard_map/ppermute | solution.py:31
  455.5 7.2 %collective-permute-done.19 = f32[1,8,1,16,128]{4,3,2,1,0:T(8,128)S(1)} collective-permute-done((f32[1,8,1,16,128]{4,3,2,1,0:T(8,128)S(1)}, f32[1,8,1,16,128]{4,3,2,1,0:T(8,128)S(1)}, u32[]{:S(2)}, u32[]{:S(2)}) %collective-permute-start.19) | collective-permute-done | bytes 65568 | tf_op jit(solution)/shard_map/ppermute | solution.py:28
  467.8 6.7 %collective-permute-done.21 = f32[1,8,1,16,128]{4,3,2,1,0:T(8,128)S(1)} collective-permute-done((f32[1,8,1,16,128]{4,3,2,1,0:T(8,128)S(1)}, f32[1,8,1,16,128]{4,3,2,1,0:T(8,128)S(1)}, u32[]{:S(2)}, u32[]{:S(2)}) %collective-permute-start.21) | collective-permute-done | bytes 65568 | tf_op jit(solution)/shard_map/ppermute | solution.py:28
  475.9 53.6 %all-gather.15.cloned.1.call-done = f32[8,8,4,16,128]{4,3,2,1,0:T(8,128)} async-done(((f32[1,8,4,16,128]{4,3,2,1,0:T(8,128)}), f32[8,8,4,16,128]{4,3,2,1,0:T(8,128)}) %all-gather.15.cloned.1.call-update) | async-done | bytes 2097168 | tf_op jit(solution)/shard_map/all_gather | solution.py:139
  529.5 4.4 fusion.2
  534.4 7.5 %collective-permute-start.22 = (f32[1,8,1,16,128]{4,3,2,1,0:T(8,128)S(1)}, f32[1,8,1,16,128]{4,3,2,1,0:T(8,128)S(1)}, u32[]{:S(2)}, u32[]{:S(2)}) collective-permute-start(f32[1,8,1,16,128]{4,3,2,1,0:T(8,128)S(1)} %get-tuple-element.73), channel_id=1, source_target_pairs={{1,0},{2,1},{3,2},{4,3},{5,4},{6,5},{7,6},{8,7},{9,8},{10,9},{11,1... | collective-permute-start | bytes 196616 | tf_op jit(solution)/shard_map/ppermute | solution.py:31
  543.9 7.2 %collective-permute-done.23 = f32[1,8,1,16,128]{4,3,2,1,0:T(8,128)S(1)} collective-permute-done((f32[1,8,1,16,128]{4,3,2,1,0:T(8,128)S(1)}, f32[1,8,1,16,128]{4,3,2,1,0:T(8,128)S(1)}, u32[]{:S(2)}, u32[]{:S(2)}) %collective-permute-start.23) | collective-permute-done | bytes 65568 | tf_op jit(solution)/shard_map/ppermute | solution.py:28
  556.3 6.7 %collective-permute-done.25 = f32[1,8,1,16,128]{4,3,2,1,0:T(8,128)S(1)} collective-permute-done((f32[1,8,1,16,128]{4,3,2,1,0:T(8,128)S(1)}, f32[1,8,1,16,128]{4,3,2,1,0:T(8,128)S(1)}, u32[]{:S(2)}, u32[]{:S(2)}) %collective-permute-start.25) | collective-permute-done | bytes 65568 | tf_op jit(solution)/shard_map/ppermute | solution.py:28
  564.0 53.9 %all-gather.17.cloned.1.call-done = f32[8,8,4,16,128]{4,3,2,1,0:T(8,128)} async-done(((f32[1,8,4,16,128]{4,3,2,1,0:T(8,128)}), f32[8,8,4,16,128]{4,3,2,1,0:T(8,128)}) %all-gather.17.cloned.1.call-update) | async-done | bytes 2097168 | tf_op jit(solution)/shard_map/all_gather | solution.py:139
  617.9 4.4 fusion
  622.9 7.5 %collective-permute-start.26 = (f32[1,8,1,16,128]{4,3,2,1,0:T(8,128)S(1)}, f32[1,8,1,16,128]{4,3,2,1,0:T(8,128)S(1)}, u32[]{:S(2)}, u32[]{:S(2)}) collective-permute-start(f32[1,8,1,16,128]{4,3,2,1,0:T(8,128)S(1)} %get-tuple-element.61), channel_id=1, source_target_pairs={{1,0},{2,1},{3,2},{4,3},{5,4},{6,5},{7,6},{8,7},{9,8},{10,9},{11,1... | collective-permute-start | bytes 196616 | tf_op jit(solution)/shard_map/ppermute | solution.py:31
  632.4 7.2 %collective-permute-done.27 = f32[1,8,1,16,128]{4,3,2,1,0:T(8,128)S(1)} collective-permute-done((f32[1,8,1,16,128]{4,3,2,1,0:T(8,128)S(1)}, f32[1,8,1,16,128]{4,3,2,1,0:T(8,128)S(1)}, u32[]{:S(2)}, u32[]{:S(2)}) %collective-permute-start.27) | collective-permute-done | bytes 65568 | tf_op jit(solution)/shard_map/ppermute | solution.py:28
  (167 shorter events, 64.3 us)
Async XLA Ops:
  6.5 76.7 %all-gather.7.cloned.1.call-start = ((), (), s32[]{:S(2)}) async-start(), calls=%async_computation | async-start | bytes 2359296 | tf_op jit(solution)/shard_map/all_gather | solution.py:139
  7.3 18.7 %collective-permute-start = (f32[8,1,16,128]{3,2,1,0:T(8,128)S(1)}, f32[8,1,16,128]{3,2,1,0:T(8,128)S(1)}, u32[]{:S(2)}, u32[]{:S(2)}) collective-permute-start(f32[8,1,16,128]{3,2,1,0:T(8,128)S(1)} %get-tuple-element.165), channel_id=1, source_target_pairs={{0,1},{1,2},{2,3},{3,4},{4,5},{5,6},{6,7},{7,8},{8,9},{9,10},{10,1... | collective-permute-start | bytes 196616 | tf_op jit(solution)/shard_map/ppermute | solution.py:28
  9.3 16.8 %collective-permute-start.1 = (f32[8,1,16,128]{3,2,1,0:T(8,128)S(1)}, f32[8,1,16,128]{3,2,1,0:T(8,128)S(1)}, u32[]{:S(2)}, u32[]{:S(2)}) collective-permute-start(f32[8,1,16,128]{3,2,1,0:T(8,128)S(1)} %get-tuple-element.166), channel_id=1, source_target_pairs={{1,0},{2,1},{3,2},{4,3},{5,4},{6,5},{7,6},{8,7},{9,8},{10,9},{11,1... | collective-permute-start | bytes 196616 | tf_op jit(solution)/shard_map/ppermute | solution.py:31
  27.5 144.4 %all-gather.9.cloned.1.call-start = ((), (), s32[]{:S(2)}) async-start(), calls=%async_computation.1 | async-start | bytes 2359296 | tf_op jit(solution)/shard_map/all_gather | solution.py:139
  27.6 60.1 %collective-permute-start.2 = (f32[1,8,1,16,128]{4,3,2,1,0:T(8,128)S(1)}, f32[1,8,1,16,128]{4,3,2,1,0:T(8,128)S(1)}, u32[]{:S(2)}, u32[]{:S(2)}) collective-permute-start(f32[1,8,1,16,128]{4,3,2,1,0:T(8,128)S(1)} %get-tuple-element.167), channel_id=1, source_target_pairs={{1,0},{2,1},{3,2},{4,3},{5,4},{6,5},{7,6},{8,7},{9,8},{10,9},{11,1... | collective-permute-start | bytes 196616 | tf_op jit(solution)/shard_map/ppermute | solution.py:31
  33.3 54.3 %collective-permute-start.3 = (f32[1,8,1,16,128]{4,3,2,1,0:T(8,128)S(1)}, f32[1,8,1,16,128]{4,3,2,1,0:T(8,128)S(1)}, u32[]{:S(2)}, u32[]{:S(2)}) collective-permute-start(f32[1,8,1,16,128]{4,3,2,1,0:T(8,128)S(1)} %get-tuple-element.168), channel_id=1, source_target_pairs={{0,1},{1,2},{2,3},{3,4},{4,5},{5,6},{6,7},{7,8},{8,9},{9,10},{10,1... | collective-permute-start | bytes 196616 | tf_op jit(solution)/shard_map/ppermute | solution.py:28
  88.4 9.5 %collective-permute-start.4 = (f32[1,8,1,16,128]{4,3,2,1,0:T(8,128)S(1)}, f32[1,8,1,16,128]{4,3,2,1,0:T(8,128)S(1)}, u32[]{:S(2)}, u32[]{:S(2)}) collective-permute-start(f32[1,8,1,16,128]{4,3,2,1,0:T(8,128)S(1)} %get-tuple-element.155), channel_id=1, source_target_pairs={{1,0},{2,1},{3,2},{4,3},{5,4},{6,5},{7,6},{8,7},{9,8},{10,9},{11,1... | collective-permute-start | bytes 196616 | tf_op jit(solution)/shard_map/ppermute | solution.py:31
  95.9 9.2 %collective-permute-start.5 = (f32[1,8,1,16,128]{4,3,2,1,0:T(8,128)S(1)}, f32[1,8,1,16,128]{4,3,2,1,0:T(8,128)S(1)}, u32[]{:S(2)}, u32[]{:S(2)}) collective-permute-start(f32[1,8,1,16,128]{4,3,2,1,0:T(8,128)S(1)} %get-tuple-element.156), channel_id=1, source_target_pairs={{0,1},{1,2},{2,3},{3,4},{4,5},{5,6},{6,7},{7,8},{8,9},{9,10},{10,1... | collective-permute-start | bytes 196616 | tf_op jit(solution)/shard_map/ppermute | solution.py:28
  105.9 4.4 collective-permute-start.6
  107.8 9.2 %collective-permute-start.7 = (f32[1,8,1,16,128]{4,3,2,1,0:T(8,128)S(1)}, f32[1,8,1,16,128]{4,3,2,1,0:T(8,128)S(1)}, u32[]{:S(2)}, u32[]{:S(2)}) collective-permute-start(f32[1,8,1,16,128]{4,3,2,1,0:T(8,128)S(1)} %get-tuple-element.146), channel_id=1, source_target_pairs={{0,1},{1,2},{2,3},{3,4},{4,5},{5,6},{6,7},{7,8},{8,9},{9,10},{10,1... | collective-permute-start | bytes 196616 | tf_op jit(solution)/shard_map/ppermute | solution.py:28
  118.0 142.3 %all-gather.11.cloned.1.call-start = ((), (), s32[]{:S(2)}) async-start(), calls=%async_computation.2 | async-start | bytes 2359296 | tf_op jit(solution)/shard_map/all_gather | solution.py:139
  176.9 9.5 %collective-permute-start.8 = (f32[1,8,1,16,128]{4,3,2,1,0:T(8,128)S(1)}, f32[1,8,1,16,128]{4,3,2,1,0:T(8,128)S(1)}, u32[]{:S(2)}, u32[]{:S(2)}) collective-permute-start(f32[1,8,1,16,128]{4,3,2,1,0:T(8,128)S(1)} %get-tuple-element.135), channel_id=1, source_target_pairs={{1,0},{2,1},{3,2},{4,3},{5,4},{6,5},{7,6},{8,7},{9,8},{10,9},{11,1... | collective-permute-start | bytes 196616 | tf_op jit(solution)/shard_map/ppermute | solution.py:31
  184.4 9.2 %collective-permute-start.9 = (f32[1,8,1,16,128]{4,3,2,1,0:T(8,128)S(1)}, f32[1,8,1,16,128]{4,3,2,1,0:T(8,128)S(1)}, u32[]{:S(2)}, u32[]{:S(2)}) collective-permute-start(f32[1,8,1,16,128]{4,3,2,1,0:T(8,128)S(1)} %get-tuple-element.136), channel_id=1, source_target_pairs={{0,1},{1,2},{2,3},{3,4},{4,5},{5,6},{6,7},{7,8},{8,9},{9,10},{10,1... | collective-permute-start | bytes 196616 | tf_op jit(solution)/shard_map/ppermute | solution.py:28
  196.2 9.2 %collective-permute-start.11 = (f32[1,8,1,16,128]{4,3,2,1,0:T(8,128)S(1)}, f32[1,8,1,16,128]{4,3,2,1,0:T(8,128)S(1)}, u32[]{:S(2)}, u32[]{:S(2)}) collective-permute-start(f32[1,8,1,16,128]{4,3,2,1,0:T(8,128)S(1)} %get-tuple-element.126), channel_id=1, source_target_pairs={{0,1},{1,2},{2,3},{3,4},{4,5},{5,6},{6,7},{7,8},{8,9},{9,10},{10,1... | collective-permute-start | bytes 196616 | tf_op jit(solution)/shard_map/ppermute | solution.py:28
  206.5 160.3 %all-reduce.2.cloned.1.call-start = ((), (), s32[]{:S(2)}) async-start(), calls=%async_computation.3 | async-start | bytes 524288 | tf_op jit(solution)/shard_map/psum | solution.py:38
  265.3 9.5 %collective-permute-start.12 = (f32[1,8,1,16,128]{4,3,2,1,0:T(8,128)S(1)}, f32[1,8,1,16,128]{4,3,2,1,0:T(8,128)S(1)}, u32[]{:S(2)}, u32[]{:S(2)}) collective-permute-start(f32[1,8,1,16,128]{4,3,2,1,0:T(8,128)S(1)} %get-tuple-element.115), channel_id=1, source_target_pairs={{1,0},{2,1},{3,2},{4,3},{5,4},{6,5},{7,6},{8,7},{9,8},{10,9},{11,1... | collective-permute-start | bytes 196616 | tf_op jit(solution)/shard_map/ppermute | solution.py:31
  272.9 9.2 %collective-permute-start.13 = (f32[1,8,1,16,128]{4,3,2,1,0:T(8,128)S(1)}, f32[1,8,1,16,128]{4,3,2,1,0:T(8,128)S(1)}, u32[]{:S(2)}, u32[]{:S(2)}) collective-permute-start(f32[1,8,1,16,128]{4,3,2,1,0:T(8,128)S(1)} %get-tuple-element.116), channel_id=1, source_target_pairs={{0,1},{1,2},{2,3},{3,4},{4,5},{5,6},{6,7},{7,8},{8,9},{9,10},{10,1... | collective-permute-start | bytes 196616 | tf_op jit(solution)/shard_map/ppermute | solution.py:28
  283.1 157.7 %all-gather.13.cloned.1.call-start = ((), (), s32[]{:S(2)}) async-start(), calls=%async_computation.4 | async-start | bytes 2359296 | tf_op jit(solution)/shard_map/all_gather | solution.py:139
  367.7 9.2 %collective-permute-start.14 = (f32[8,1,16,128]{3,2,1,0:T(8,128)S(1)}, f32[8,1,16,128]{3,2,1,0:T(8,128)S(1)}, u32[]{:S(2)}, u32[]{:S(2)}) collective-permute-start(f32[8,1,16,128]{3,2,1,0:T(8,128)S(1)} %get-tuple-element.103), channel_id=1, source_target_pairs={{0,1},{1,2},{2,3},{3,4},{4,5},{5,6},{6,7},{7,8},{8,9},{9,10},{10,1... | collective-permute-start | bytes 196616 | tf_op jit(solution)/shard_map/ppermute | solution.py:28
  369.6 9.1 %collective-permute-start.15 = (f32[8,1,16,128]{3,2,1,0:T(8,128)S(1)}, f32[8,1,16,128]{3,2,1,0:T(8,128)S(1)}, u32[]{:S(2)}, u32[]{:S(2)}) collective-permute-start(f32[8,1,16,128]{3,2,1,0:T(8,128)S(1)} %get-tuple-element.104), channel_id=1, source_target_pairs={{1,0},{2,1},{3,2},{4,3},{5,4},{6,5},{7,6},{8,7},{9,8},{10,9},{11,1... | collective-permute-start | bytes 196616 | tf_op jit(solution)/shard_map/ppermute | solution.py:31
  381.2 148.3 %all-gather.15.cloned.1.call-start = ((), (), s32[]{:S(2)}) async-start(), calls=%async_computation.5 | async-start | bytes 2359296 | tf_op jit(solution)/shard_map/all_gather | solution.py:139
  381.3 64.0 %collective-permute-start.16 = (f32[1,8,1,16,128]{4,3,2,1,0:T(8,128)S(1)}, f32[1,8,1,16,128]{4,3,2,1,0:T(8,128)S(1)}, u32[]{:S(2)}, u32[]{:S(2)}) collective-permute-start(f32[1,8,1,16,128]{4,3,2,1,0:T(8,128)S(1)} %get-tuple-element.105), channel_id=1, source_target_pairs={{1,0},{2,1},{3,2},{4,3},{5,4},{6,5},{7,6},{8,7},{9,8},{10,9},{11,1... | collective-permute-start | bytes 196616 | tf_op jit(solution)/shard_map/ppermute | solution.py:31
  388.6 56.7 %collective-permute-start.17 = (f32[1,8,1,16,128]{4,3,2,1,0:T(8,128)S(1)}, f32[1,8,1,16,128]{4,3,2,1,0:T(8,128)S(1)}, u32[]{:S(2)}, u32[]{:S(2)}) collective-permute-start(f32[1,8,1,16,128]{4,3,2,1,0:T(8,128)S(1)} %get-tuple-element.106), channel_id=1, source_target_pairs={{0,1},{1,2},{2,3},{3,4},{4,5},{5,6},{6,7},{7,8},{8,9},{9,10},{10,1... | collective-permute-start | bytes 196616 | tf_op jit(solution)/shard_map/ppermute | solution.py:28
  446.0 9.5 %collective-permute-start.18 = (f32[1,8,1,16,128]{4,3,2,1,0:T(8,128)S(1)}, f32[1,8,1,16,128]{4,3,2,1,0:T(8,128)S(1)}, u32[]{:S(2)}, u32[]{:S(2)}) collective-permute-start(f32[1,8,1,16,128]{4,3,2,1,0:T(8,128)S(1)} %get-tuple-element.93), channel_id=1, source_target_pairs={{1,0},{2,1},{3,2},{4,3},{5,4},{6,5},{7,6},{8,7},{9,8},{10,9},{11,1... | collective-permute-start | bytes 196616 | tf_op jit(solution)/shard_map/ppermute | solution.py:31
  453.5 9.2 %collective-permute-start.19 = (f32[1,8,1,16,128]{4,3,2,1,0:T(8,128)S(1)}, f32[1,8,1,16,128]{4,3,2,1,0:T(8,128)S(1)}, u32[]{:S(2)}, u32[]{:S(2)}) collective-permute-start(f32[1,8,1,16,128]{4,3,2,1,0:T(8,128)S(1)} %get-tuple-element.94), channel_id=1, source_target_pairs={{0,1},{1,2},{2,3},{3,4},{4,5},{5,6},{6,7},{7,8},{8,9},{9,10},{10,1... | collective-permute-start | bytes 196616 | tf_op jit(solution)/shard_map/ppermute | solution.py:28
  465.4 9.2 %collective-permute-start.21 = (f32[1,8,1,16,128]{4,3,2,1,0:T(8,128)S(1)}, f32[1,8,1,16,128]{4,3,2,1,0:T(8,128)S(1)}, u32[]{:S(2)}, u32[]{:S(2)}) collective-permute-start(f32[1,8,1,16,128]{4,3,2,1,0:T(8,128)S(1)} %get-tuple-element.84), channel_id=1, source_target_pairs={{0,1},{1,2},{2,3},{3,4},{4,5},{5,6},{6,7},{7,8},{8,9},{9,10},{10,1... | collective-permute-start | bytes 196616 | tf_op jit(solution)/shard_map/ppermute | solution.py:28
  475.6 142.3 %all-gather.17.cloned.1.call-start = ((), (), s32[]{:S(2)}) async-start(), calls=%async_computation.6 | async-start | bytes 2359296 | tf_op jit(solution)/shard_map/all_gather | solution.py:139
  534.4 9.5 %collective-permute-start.22 = (f32[1,8,1,16,128]{4,3,2,1,0:T(8,128)S(1)}, f32[1,8,1,16,128]{4,3,2,1,0:T(8,128)S(1)}, u32[]{:S(2)}, u32[]{:S(2)}) collective-permute-start(f32[1,8,1,16,128]{4,3,2,1,0:T(8,128)S(1)} %get-tuple-element.73), channel_id=1, source_target_pairs={{1,0},{2,1},{3,2},{4,3},{5,4},{6,5},{7,6},{8,7},{9,8},{10,9},{11,1... | collective-permute-start | bytes 196616 | tf_op jit(solution)/shard_map/ppermute | solution.py:31
  542.0 9.2 %collective-permute-start.23 = (f32[1,8,1,16,128]{4,3,2,1,0:T(8,128)S(1)}, f32[1,8,1,16,128]{4,3,2,1,0:T(8,128)S(1)}, u32[]{:S(2)}, u32[]{:S(2)}) collective-permute-start(f32[1,8,1,16,128]{4,3,2,1,0:T(8,128)S(1)} %get-tuple-element.74), channel_id=1, source_target_pairs={{0,1},{1,2},{2,3},{3,4},{4,5},{5,6},{6,7},{7,8},{8,9},{9,10},{10,1... | collective-permute-start | bytes 196616 | tf_op jit(solution)/shard_map/ppermute | solution.py:28
  553.8 9.2 %collective-permute-start.25 = (f32[1,8,1,16,128]{4,3,2,1,0:T(8,128)S(1)}, f32[1,8,1,16,128]{4,3,2,1,0:T(8,128)S(1)}, u32[]{:S(2)}, u32[]{:S(2)}) collective-permute-start(f32[1,8,1,16,128]{4,3,2,1,0:T(8,128)S(1)} %get-tuple-element.64), channel_id=1, source_target_pairs={{0,1},{1,2},{2,3},{3,4},{4,5},{5,6},{6,7},{7,8},{8,9},{9,10},{10,1... | collective-permute-start | bytes 196616 | tf_op jit(solution)/shard_map/ppermute | solution.py:28
  622.9 9.5 %collective-permute-start.26 = (f32[1,8,1,16,128]{4,3,2,1,0:T(8,128)S(1)}, f32[1,8,1,16,128]{4,3,2,1,0:T(8,128)S(1)}, u32[]{:S(2)}, u32[]{:S(2)}) collective-permute-start(f32[1,8,1,16,128]{4,3,2,1,0:T(8,128)S(1)} %get-tuple-element.61), channel_id=1, source_target_pairs={{1,0},{2,1},{3,2},{4,3},{5,4},{6,5},{7,6},{8,7},{9,8},{10,9},{11,1... | collective-permute-start | bytes 196616 | tf_op jit(solution)/shard_map/ppermute | solution.py:31
  630.4 9.2 %collective-permute-start.27 = (f32[1,8,1,16,128]{4,3,2,1,0:T(8,128)S(1)}, f32[1,8,1,16,128]{4,3,2,1,0:T(8,128)S(1)}, u32[]{:S(2)}, u32[]{:S(2)}) collective-permute-start(f32[1,8,1,16,128]{4,3,2,1,0:T(8,128)S(1)} %get-tuple-element.62), channel_id=1, source_target_pairs={{0,1},{1,2},{2,3},{3,4},{4,5},{5,6},{6,7},{7,8},{8,9},{9,10},{10,1... | collective-permute-start | bytes 196616 | tf_op jit(solution)/shard_map/ppermute | solution.py:28
  (12 other events, 411.7 us)
Sparse Core Ops, SparseCore 0:
  27.6 55.5 all-gather.6
  118.1 53.7 all-gather.8
  206.6 53.7 all-gather.10
  283.3 83.4 all-reduce.1
  381.3 59.4 all-gather.12
  475.7 53.7 all-gather.14
  564.2 53.7 all-gather.16
where the time goes:
time: 649 us; the launch traced here: 648 us
  waiting for transfers between devices  468 us (72%)
  starting transfers between devices  116 us (18%)
  matrix products  26.6 us (4%)
  between operations  16 us (2%)
  other arithmetic  13.8 us (2%)
  local copies, waits for them, and re-layouts  6.91 us (1%)
    all_gather x6, waiting for transfers between devices, on_device(): piece = lax.all_gather(rates, 'node', axis=0, tiled=True)  312 us
    ppermute x14, starting transfers between devices, with_halo(): lax.ppermute(lax.slice_in_dim(block, 0, width, axis=dim), axis, backward)  86.4 us
    psum x1, waiting for transfers between devices, broadcast(): return lax.psum(block, axis)  83.6 us
    ppermute x14, waiting for transfers between devices, with_halo(): lax.ppermute(lax.slice_in_dim(block, block.shape[dim] - width, None, axis...  70.3 us
    ppermute x14, starting transfers between devices, with_halo(): lax.ppermute(lax.slice_in_dim(block, block.shape[dim] - width, None, axis...  28.8 us
    dot_general x6, matrix products, on_device(): jnp.tensordot(coefs, piece, axes=1, precision=lax.Precision.HIGHEST)  26.6 us
  transfers between devices with their start and end apart: 35, of which 18 were waited for; matrix products, arithmetic and copies ran while one was open for 2% of the time, Pallas kernels for 0%

commit v1 on v0

--- a/solution.py
+++ b/solution.py
@@ -1,9 +1,12 @@
+import functools
 import math
 
 import jax
 import jax.numpy as jnp
 import numpy as np
 from jax import lax
+from jax.experimental import pallas as pl
+from jax.experimental.pallas import tpu as pltpu
 from jax.sharding import PartitionSpec as P
 
 P_SIZE = 8
@@ -19,23 +22,29 @@
 activation = 3.0
 
 
-def with_halo(block, sides, width):
-    for axis, dim in sides:
-        count = lax.axis_size(axis)
-        forward = [(i, i + 1) for i in range(count - 1)]
-        forward.append((count - 1, 0))
-        backward = [(target, source) for source, target in forward]
-        low = lax.ppermute(
-            lax.slice_in_dim(block, block.shape[dim] - width, None, axis=dim), axis, forward
-        )
-        high = lax.ppermute(lax.slice_in_dim(block, 0, width, axis=dim), axis, backward)
-        block = jnp.concatenate([low, block, high], axis=dim)
-    return block
-
-
-def broadcast(block, axis, source):
-    block = jnp.where(lax.axis_index(axis) == source, block, jnp.zeros_like(block))
-    return lax.psum(block, axis)
+def gather_halo(block, dim, width):
+    axis = "space"
+    count = lax.axis_size(axis)
+    size = block.shape[dim]
+    lows = []
+    highs = []
+    distance = 1
+    left = width
+    while left > 0:
+        take = min(size, left)
+        up = [(i, (i + distance) % count) for i in range(count)]
+        down = [(i, (i - distance) % count) for i in range(count)]
+        lows.insert(0, lax.ppermute(lax.slice_in_dim(block, size - take, size, axis=dim), axis, up))
+        highs.append(lax.ppermute(lax.slice_in_dim(block, 0, take, axis=dim), axis, down))
+        left -= take
+        distance += 1
+    return jnp.concatenate(lows + [block] + highs, axis=dim)
+
+
+def trim(block, count, dim=-3):
+    if count == 0:
+        return block
+    return lax.slice_in_dim(block, count, block.shape[dim] - count, axis=dim)
 
 
 def legendre_pair(count, point):
@@ -117,41 +126,201 @@
     return (goal + factor * (near_sum(extended) - drive(inner))) / (1.0 + 6.0 * factor)
 
 
+def plane_near(below, center, above):
+    result = above + below
+    result = result + pltpu.roll(center, center.shape[1] - 1, 1) + pltpu.roll(center, 1, 1)
+    return result + pltpu.roll(center, center.shape[2] - 1, 2) + pltpu.roll(center, 1, 2)
+
+
+def plane_drive(field):
+    squares = field * field
+    total = jnp.sum(squares, axis=0, keepdims=True)
+    return -field + squares * field + 2.0 * cross_coef * field * (total - squares)
+
+
+def prep_kernel(start_ref, bracket_ref, pull_ref):
+    def body(z, carry):
+        center = start_ref[:, z + 1]
+        near = plane_near(start_ref[:, z], center, start_ref[:, z + 2])
+        push = plane_drive(center)
+        bracket_ref[:, z] = push - (near - 6.0 * center)
+        pull_ref[:, z] = near - push
+        return carry
+
+    lax.fori_loop(0, bracket_ref.shape[1], body, 0)
+
+
+def prep_call(start):
+    count, planes, rows, lanes = start.shape
+    shape = jax.ShapeDtypeStruct((count, planes - 2, rows, lanes), jnp.float32)
+    return pl.pallas_call(
+        prep_kernel,
+        out_shape=(shape, shape),
+        in_specs=[pl.BlockSpec(memory_space=pltpu.VMEM)],
+        out_specs=(pl.BlockSpec(memory_space=pltpu.VMEM), pl.BlockSpec(memory_space=pltpu.VMEM)),
+    )(start)
+
+
+def sweep_kernel(
+    sel_ref, coef_ref, state_ref, rates_ref, start_ref, fac_ref, mob_ref, *rest,
+    halo, depth, first, with_rates, jacobi
+):
+    if with_rates:
+        out_ref, out_rates_ref, goal_sc, *bufs = rest
+    else:
+        out_ref, goal_sc, *bufs = rest
+        out_rates_ref = None
+    node = sel_ref[pl.program_id(0)]
+    count = rates_ref.shape[0]
+    dt_tau = time_step * coef_ref[node, count]
+    weights = [coef_ref[node, j] for j in range(count)]
+    goal_planes = goal_sc.shape[1]
+    off_goal = depth - (halo - 1)
+
+    def goal_body(z, carry):
+        acc = rates_ref[0, :, z] * weights[0]
+        for j in range(1, count):
+            acc = acc + rates_ref[j, :, z] * weights[j]
+        goal_sc[:, z] = start_ref[:, z + off_goal] + time_step * acc - dt_tau * rates_ref[node, :, z]
+        return carry
+
+    lax.fori_loop(0, goal_planes, goal_body, 0)
+
+    source = None
+    for index in range(jacobi):
+        target = out_ref if index + 1 == jacobi else bufs[index % len(bufs)]
+        planes = goal_planes - 2 * index
+        off_fac = depth - (halo - 1 - index)
+
+        if index == 0 and first:
+            def body(z, carry, target=target, off_fac=off_fac):
+                f = fac_ref[0, :, z + off_fac]
+                target_view = target.at[0] if target is out_ref else target
+                target_view[:, z] = (goal_sc[:, z] + f * state_ref[:, z]) / (1.0 + 6.0 * f)
+                return carry
+        else:
+            def body(z, carry, target=target, off_fac=off_fac, source=source, index=index):
+                if source is None:
+                    src = state_ref.at[0]
+                else:
+                    src = source
+                f = fac_ref[0, :, z + off_fac]
+                center = src[:, z + 1]
+                near = plane_near(src[:, z], center, src[:, z + 2])
+                value = (goal_sc[:, z + index] + f * (near - plane_drive(center))) / (1.0 + 6.0 * f)
+                target_view = target.at[0] if target is out_ref else target
+                target_view[:, z] = value
+                return carry
+
+        lax.fori_loop(0, planes, body, 0)
+        source = target.at[0] if target is out_ref else target
+
+    if with_rates:
+        final_halo = halo - jacobi
+        off_mob = depth - (final_halo - 1)
+
+        def rate_body(z, carry):
+            src = out_ref.at[0]
+            mob = mob_ref[0, :, z + off_mob]
+            center = src[:, z + 1]
+            near = plane_near(src[:, z], center, src[:, z + 2])
+            out_rates_ref[0, :, z] = -mob * (plane_drive(center) - (near - 6.0 * center))
+            return carry
+
+        lax.fori_loop(0, out_rates_ref.shape[2], rate_body, 0)
+
+
+def sweep_call(sel, coef, state, rates, start, factor, mobility, halo, depth, first, with_rates):
+    count, order, goal_planes, rows, lanes = rates.shape
+    picks = sel.shape[0]
+    out_planes = goal_planes - 2 * (JACOBI - 1)
+    whole5 = lambda i, sel_ref: (0, 0, 0, 0, 0)
+    whole4 = lambda i, sel_ref: (0, 0, 0, 0)
+    per_node = lambda i, sel_ref: (sel_ref[i], 0, 0, 0, 0)
+    per_out = lambda i, sel_ref: (i, 0, 0, 0, 0)
+    if first:
+        state_spec = pl.BlockSpec(state.shape, whole4)
+    else:
+        state_spec = pl.BlockSpec((1,) + state.shape[1:], per_node)
+    in_specs = [
+        pl.BlockSpec(memory_space=pltpu.SMEM),
+        state_spec,
+        pl.BlockSpec(rates.shape, whole5),
+        pl.BlockSpec(start.shape, whole4),
+        pl.BlockSpec((1,) + factor.shape[1:], per_node),
+        pl.BlockSpec((1,) + mobility.shape[1:], per_node),
+    ]
+    out_shape = [jax.ShapeDtypeStruct((picks, order, out_planes, rows, lanes), jnp.float32)]
+    out_specs = [pl.BlockSpec((1, order, out_planes, rows, lanes), per_out)]
+    if with_rates:
+        out_shape.append(jax.ShapeDtypeStruct((picks, order, out_planes - 2, rows, lanes), jnp.float32))
+        out_specs.append(pl.BlockSpec((1, order, out_planes - 2, rows, lanes), per_out))
+    scratch = [pltpu.VMEM((order, goal_planes, rows, lanes), jnp.float32)]
+    scratch += [pltpu.VMEM((order, goal_planes, rows, lanes), jnp.float32) for _ in range(min(2, JACOBI - 1))]
+    kernel = functools.partial(
+        sweep_kernel, halo=halo, depth=depth, first=first, with_rates=with_rates, jacobi=JACOBI
+    )
+    result = pl.pallas_call(
+        kernel,
+        out_shape=tuple(out_shape),
+        grid_spec=pltpu.PrefetchScalarGridSpec(
+            num_scalar_prefetch=1,
+            grid=(picks,),
+            in_specs=in_specs,
+            out_specs=tuple(out_specs),
+            scratch_shapes=scratch,
+        ),
+        compiler_params=pltpu.CompilerParams(vmem_limit_bytes=60 * 1024 * 1024),
+    )(sel, coef, state, rates, start, factor, mobility)
+    return result
+
+
 def on_device(grain_ids, peak_heat):
     total_nodes = lax.axis_size("node") * NODE_DEV
     node_times, table = radau_table(total_nodes)
-    weights = jnp.asarray(table, jnp.float32)
-    first = lax.axis_index("node") * NODE_DEV
-    times = lax.dynamic_slice_in_dim(jnp.asarray(node_times, jnp.float32), first, NODE_DEV, 0)
-    my_rows = lax.dynamic_slice_in_dim(weights, first, NODE_DEV, 0)
-    taus = times.reshape((NODE_DEV, 1, 1, 1, 1))
+    times = jnp.asarray(node_times, jnp.float32)
+    taus = times.reshape((total_nodes, 1, 1, 1, 1))
+    coef = jnp.asarray(
+        np.concatenate([table, node_times[:, None]], axis=1).astype(np.float32)
+    )
+    mine = lax.axis_index("node") * NODE_DEV
+    depth = SWEEPS * JACOBI
     orders = jnp.arange(P_SIZE, dtype=jnp.int32)
-    start = (grain_ids[None] == orders[:, None, None, None]).astype(jnp.float32)
+    every = jnp.arange(total_nodes, dtype=jnp.int32)
+
+    packed = jnp.stack([grain_ids.astype(jnp.float32), peak_heat])
+    packed = gather_halo(packed, 1, depth)
+    ids_wide = packed[0]
+    peak_wide = packed[1]
+    start = (ids_wide[None] == orders[:, None, None, None].astype(jnp.float32)).astype(jnp.float32)
+
     states = None
     for step_index in range(STEPS):
+        last_step = step_index + 1 == STEPS
         moments = (step_index + times) * time_step
-        mobility = heat_mobility(peak_heat[None], moments[:, None, None, None])[:, None]
+        mobility = heat_mobility(peak_wide[None], moments[:, None, None, None])[:, None]
         factor = time_step * taus * mobility
-        start_wide = with_halo(start, (("space", 1),), 1)
-        rates = rate_on(start_wide[None], mobility)
-        states = jnp.broadcast_to(start[None], rates.shape)
+        bracket, pull = prep_call(start)
+        rates = -trim(mobility, 1) * bracket[None]
+        halo = depth
+        states = pull
         for sweep_index in range(SWEEPS):
-            piece = lax.all_gather(rates, "node", axis=0, tiled=True)
-            coefs = lax.slice_in_dim(my_rows, 0, piece.shape[0], axis=1)
-            quad = jnp.zeros_like(rates) + jnp.tensordot(
-                coefs, piece, axes=1, precision=lax.Precision.HIGHEST
+            last = sweep_index + 1 == SWEEPS
+            if last:
+                keep = mine if last_step else total_nodes - 1
+                sel = jnp.reshape(jnp.asarray(keep, jnp.int32), (1,))
+            else:
+                sel = every
+            outs = sweep_call(
+                sel, coef, states, rates, start, factor, mobility,
+                halo, depth, sweep_index == 0, not last,
             )
-            goal = start[None] + time_step * quad - time_step * taus * rates
-            last = sweep_index + 1 == SWEEPS
-            passes = JACOBI if last else JACOBI + 1
-            for relax_index in range(passes):
-                extended = with_halo(states, (("space", 2),), 1)
-                if relax_index < JACOBI:
-                    states = relax_on(extended, goal, factor)
-                else:
-                    rates = rate_on(extended, mobility)
-        if step_index + 1 < STEPS:
-            start = broadcast(states[-1], "node", lax.axis_size("node") - 1)
+            states = outs[0]
+            if not last:
+                rates = outs[1]
+            halo -= JACOBI
+        if not last_step:
+            start = gather_halo(states[0], 1, depth)
     return states
 
 

time: 649 us -> 209 us (0.32)
  waiting for transfers between devices: 468 us -> 2.11 us
  Pallas kernels: 0 us -> 140 us
  starting transfers between devices: 116 us -> 43.3 us
  matrix products: 26.6 us -> 0 us
  between operations: 16 us -> 0.18 us
    all_gather x6 -> x0, waiting for transfers between devices: 312 us -> none  [on_device(): piece = lax.all_gather(rates, 'node', axis=0, tiled=True)]
    pallas_call x0 -> x8, Pallas kernels: none -> 140 us  [the longest x6 132 us: sweep_call(): pl.pallas_call(kernel, out_shape=tuple(out_shape), grid_spec=pltpu.Prefet...]
    psum x1 -> x0, waiting for transfers between devices: 83.6 us -> none  [broadcast(): return lax.psum(block, axis)]
    ppermute x28 -> x8, starting transfers between devices: 115 us -> 43.3 us  [the longest x4 35.6 us: gather_halo(): lax.ppermute(lax.slice_in_dim(block, 0, take, axis=dim), axis, down)]
    ppermute x28 -> x8, waiting for transfers between devices: 72.2 us -> 2.11 us  [the longest x4 1.06 us: gather_halo(): lax.ppermute(lax.slice_in_dim(block, 0, take, axis=dim), axis, down)]
    dot_general x6 -> x0, matrix products: 26.6 us -> none  [on_device(): jnp.tensordot(coefs, piece, axes=1, precision=lax.Precision.HIGHEST)]
    mul x6, other arithmetic: 6.01 us -> 13 us  [the longest x4 10.2 us: on_device(): rates = -trim(mobility, 1) * bracket[None]]
  transfers between devices with their start and end apart: 35 -> 8, of which waited for: 18 -> 3; matrix products, arithmetic and copies ran while one was open for 2% -> 1% of each run, Pallas kernels for 0% -> 0%
where the time goes in v1:
time: 209 us; the launch traced here: 208 us
  Pallas kernels  140 us (67%)
  starting transfers between devices  43.3 us (21%)
  other arithmetic  17.4 us (8%)
  local copies, waits for them, and re-layouts  5.06 us (2%)
  waiting for transfers between devices  2.11 us (1%)
    pallas_call x6, Pallas kernels, sweep_call(): pl.pallas_call(kernel, out_shape=tuple(out_shape), grid_spec=pltpu.Prefet...  132 us
    ppermute x4, starting transfers between devices, gather_halo(): lax.ppermute(lax.slice_in_dim(block, 0, take, axis=dim), axis, down)  35.6 us
    mul x4, other arithmetic, on_device(): rates = -trim(mobility, 1) * bracket[None]  10.2 us
    pallas_call x2, Pallas kernels, prep_call(): pl.pallas_call(prep_kernel, out_shape=(shape, shape), in_specs=[pl.BlockS...  8.03 us
    ppermute x4, starting transfers between devices, gather_halo(): lax.ppermute(lax.slice_in_dim(block, size - take, size, axis=dim), axis, up)  7.66 us
  transfers between devices with their start and end apart: 8, of which 3 were waited for; matrix products, arithmetic and copies ran while one was open for 1% of the time, Pallas kernels for 0%

profile of v1, /device:TPU:24, one launch (start us, length us, event | category | flops | bytes accessed | tf_op | source)
XLA Modules:
  0.0 208.3 jit_solution(2709479554492419919)
XLA Ops:
  0.0 0.8 convert_bitcast_fusion
  0.8 0.8 pad_maximum_fusion
  1.5 1.9 collective-permute-start.1
  3.4 13.3 %collective-permute-start.2 = (f32[2,4,16,128]{3,2,1,0:T(8,128)S(1)}, f32[2,4,16,128]{3,2,1,0:T(8,128)S(1)}, u32[]{:S(2)}, u32[]{:S(2)}) collective-permute-start(f32[2,4,16,128]{3,2,1,0:T(8,128)S(1)} %pad_maximum_fusion), channel_id=1, source_target_pairs={{0,63},{1,0},{2,1},{3,2},{4,3},{5,4},{6,5},{7,6},{8,7},{9,8},{10,9... | collective-permute-start | bytes 196616 | tf_op jit(solution)/shard_map/ppermute | solution.py:38
  16.8 0.7 fusion.4
  17.5 1.9 collective-permute-start
  19.4 7.5 %collective-permute-start.3 = (f32[2,2,16,128]{3,2,1,0:T(8,128)S(1)}, f32[2,2,16,128]{3,2,1,0:T(8,128)S(1)}, u32[]{:S(2)}, u32[]{:S(2)}) collective-permute-start(f32[2,2,16,128]{3,2,1,0:T(8,128)S(1)} %get-tuple-element.37), channel_id=1, source_target_pairs={{0,62},{1,63},{2,0},{3,1},{4,2},{5,3},{6,4},{7,5},{8,6},{9,7},{10,... | collective-permute-start | bytes 98312 | tf_op jit(solution)/shard_map/ppermute | solution.py:38
  27.0 0.8 constant_dynamic-update-slice_fusion.2
  27.8 0.7 collective-permute-done.3
  28.6 2.8 %broadcast_multiply_fusion.2 = (f32[8,1,16,16,128]{4,3,2,1,0:T(8,128)}, f32[8,1,16,16,128]{4,3,2,1,0:T(8,128)S(1)}, f32[8,1,16,16,128]{4,3,2,1,0:T(8,128)}, f32[8,1,16,16,128]{4,3,2,1,0:T(8,128)S(1)}) fusion(f32[8]{0:T(128)} %constant.36, f32[8]{0:T(128)} %constant.48, f32[16,16,128]{2,1,0:T(8,128)S(1)} %get-tuple-element.31, f32[8]{0:T(128)} %constant.41), kind=kLoop, calls=%fused_computation.9 | loop fusion | flops 3145728 | bytes 4325472 | tf_op jit(solution)/shard_map/mul | solution.py:302
  31.4 1.4 compare_convert_fusion.start_ref
  32.8 4.1 %shard_map.46 = (f32[8,14,16,128]{3,2,1,0:T(8,128)}, f32[8,14,16,128]{3,2,1,0:T(8,128)}) custom-call(f32[8,16,16,128]{3,2,1,0:T(8,128)} %compare_convert_fusion.start_ref), custom_call_target="tpu_custom_call" | custom-call | tf_op jit(solution)/shard_map/pallas_call | solution.py:156
  36.8 5.0 %broadcast_multiply_fusion.1.rates_ref = f32[8,8,14,16,128]{4,3,2,1,0:T(8,128)} fusion(f32[8,14,16,128]{3,2,1,0:T(8,128)} %get-tuple-element.18, f32[8,14,16,128]{3,2,1,0:T(8,128)S(1)} %fusion.1), kind=kLoop, calls=%fused_computation.1 | loop fusion | flops 1835008 | bytes 9175040 | tf_op jit(solution)/shard_map/mul | solution.py:304
  41.9 0.5 iota.17.sel_ref
  42.4 32.0 %shard_map.47 = (f32[8,8,12,16,128]{4,3,2,1,0:T(8,128)}, f32[8,8,10,16,128]{4,3,2,1,0:T(8,128)}) custom-call(s32[8]{0:T(128)} %iota.17.sel_ref, f32[8,9]{1,0:T(8,128)} %constant.33.clone.coef_ref, f32[8,14,16,128]{3,2,1,0:T(8,128)} %get-tuple-element.17.state_ref, f32[8,8,14,16,128]{4,3,2,1,0:T(8,128)} %broadcast_multiply_fusion.1.rates_ref, ...), custom_call_target="tpu_custom_call" | custom-call | tf_op jit(solution)/shard_map/pallas_call | solution.py:263
  74.9 29.7 %shard_map.48 = (f32[8,8,8,16,128]{4,3,2,1,0:T(8,128)}, f32[8,8,6,16,128]{4,3,2,1,0:T(8,128)}) custom-call(s32[8]{0:T(128)} %iota.16.sel_ref, f32[8,9]{1,0:T(8,128)} %constant.33.clone.coef_ref, f32[8,8,12,16,128]{4,3,2,1,0:T(8,128)} %get-tuple-element.19.state_ref, f32[8,8,10,16,128]{4,3,2,1,0:T(8,128)} %get-tuple-element.20.rates_ref, ...), custom_call_target="tpu_custom_call" | custom-call | tf_op jit(solution)/shard_map/pallas_call | solution.py:263
  104.6 4.5 %shard_map.49 = f32[1,8,4,16,128]{4,3,2,1,0:T(8,128)} custom-call(s32[1]{0:T(128)} %constant.10.clone.1.sel_ref, f32[8,9]{1,0:T(8,128)} %constant.33.clone.coef_ref, f32[8,8,8,16,128]{4,3,2,1,0:T(8,128)} %get-tuple-element.21.state_ref, f32[8,8,6,16,128]{4,3,2,1,0:T(8,128)} %get-tuple-element.22.rates_ref, f32[8,16,16,128]{3,2,1,0:T(8,128)} %compare_convert_fusion.start_ref, ...), custom_call_target="tpu_custom_call" | custom-call | tf_op jit(solution)/shard_map/pallas_call | solution.py:263
  109.0 1.0 fusion.5
  110.0 1.9 collective-permute-start.5
  111.9 7.3 %collective-permute-start.6 = (f32[8,4,16,128]{3,2,1,0:T(8,128)}, f32[8,4,16,128]{3,2,1,0:T(8,128)S(1)}, u32[]{:S(2)}, u32[]{:S(2)}) collective-permute-start(f32[8,4,16,128]{3,2,1,0:T(8,128)} %bitcast.16), channel_id=1, source_target_pairs={{0,63},{1,0},{2,1},{3,2},{4,3},{5,4},{6,5},{7,6},{8,7},{9,8},{10,9... | collective-permute-start | bytes 786440 | tf_op jit(solution)/shard_map/ppermute | solution.py:38
  119.2 1.9 collective-permute-start.4
  121.1 7.5 %collective-permute-start.7 = (f32[8,2,16,128]{3,2,1,0:T(8,128)S(1)}, f32[8,2,16,128]{3,2,1,0:T(8,128)S(1)}, u32[]{:S(2)}, u32[]{:S(2)}) collective-permute-start(f32[8,2,16,128]{3,2,1,0:T(8,128)S(1)} %get-tuple-element.29), channel_id=1, source_target_pairs={{0,62},{1,63},{2,0},{3,1},{4,2},{5,3},{6,4},{7,5},{8,6},{9,7},{10,... | collective-permute-start | bytes 393224 | tf_op jit(solution)/shard_map/ppermute | solution.py:38
  128.8 1.0 collective-permute-done.4
  129.8 1.0 constant_dynamic-update-slice_fusion.7
  131.2 1.0 copy-done.2
  132.2 4.0 %shard_map.50 = (f32[8,14,16,128]{3,2,1,0:T(8,128)}, f32[8,14,16,128]{3,2,1,0:T(8,128)}) custom-call(f32[8,16,16,128]{3,2,1,0:T(8,128)} %copy-done.2), custom_call_target="tpu_custom_call" | custom-call | tf_op jit(solution)/shard_map/pallas_call | solution.py:156
  136.1 5.0 %broadcast_multiply_fusion.rates_ref = f32[8,8,14,16,128]{4,3,2,1,0:T(8,128)} fusion(f32[8,14,16,128]{3,2,1,0:T(8,128)} %get-tuple-element.24, f32[8,14,16,128]{3,2,1,0:T(8,128)S(1)} %fusion), kind=kLoop, calls=%fused_computation | loop fusion | flops 1835008 | bytes 9175040 | tf_op jit(solution)/shard_map/mul | solution.py:304
  141.2 0.5 iota.15.sel_ref
  141.7 32.0 %shard_map.51 = (f32[8,8,12,16,128]{4,3,2,1,0:T(8,128)}, f32[8,8,10,16,128]{4,3,2,1,0:T(8,128)}) custom-call(s32[8]{0:T(128)} %iota.15.sel_ref, f32[8,9]{1,0:T(8,128)} %constant.33.clone.coef_ref, f32[8,14,16,128]{3,2,1,0:T(8,128)} %get-tuple-element.23.state_ref, f32[8,8,14,16,128]{4,3,2,1,0:T(8,128)} %broadcast_multiply_fusion.rates_ref, ...), custom_call_target="tpu_custom_call" | custom-call | tf_op jit(solution)/shard_map/pallas_call | solution.py:263
  173.7 0.5 iota.14.sel_ref
  174.2 29.7 %shard_map.52 = (f32[8,8,8,16,128]{4,3,2,1,0:T(8,128)}, f32[8,8,6,16,128]{4,3,2,1,0:T(8,128)}) custom-call(s32[8]{0:T(128)} %iota.14.sel_ref, f32[8,9]{1,0:T(8,128)} %constant.33.clone.coef_ref, f32[8,8,12,16,128]{4,3,2,1,0:T(8,128)} %get-tuple-element.25.state_ref, f32[8,8,10,16,128]{4,3,2,1,0:T(8,128)} %get-tuple-element.26.rates_ref, ...), custom_call_target="tpu_custom_call" | custom-call | tf_op jit(solution)/shard_map/pallas_call | solution.py:263
  203.8 4.5 %shard_map.53 = f32[1,8,4,16,128]{4,3,2,1,0:T(8,128)} custom-call(s32[1]{0:T(128)} %bitcast.sel_ref, f32[8,9]{1,0:T(8,128)} %constant.33.clone.coef_ref, f32[8,8,8,16,128]{4,3,2,1,0:T(8,128)} %get-tuple-element.27.state_ref, f32[8,8,6,16,128]{4,3,2,1,0:T(8,128)} %get-tuple-element.28.rates_ref, f32[8,16,16,128]{3,2,1,0:T(8,128)} %copy-done.2, ...), custom_call_target="tpu_custom_call" | custom-call | tf_op jit(solution)/shard_map/pallas_call | solution.py:263
  (24 shorter events, 1.2 us)
Async XLA Ops:
  1.5 25.5 %collective-permute-start.1 = (f32[2,4,16,128]{3,2,1,0:T(8,128)S(1)}, f32[2,4,16,128]{3,2,1,0:T(8,128)S(1)}, u32[]{:S(2)}, u32[]{:S(2)}) collective-permute-start(f32[2,4,16,128]{3,2,1,0:T(8,128)S(1)} %pad_maximum_fusion), channel_id=1, source_target_pairs={{0,1},{1,2},{2,3},{3,4},{4,5},{5,6},{6,7},{7,8},{8,9},{9,10},{10,1... | collective-permute-start | bytes 196616 | tf_op jit(solution)/shard_map/ppermute | solution.py:37
  3.4 24.4 %collective-permute-start.2 = (f32[2,4,16,128]{3,2,1,0:T(8,128)S(1)}, f32[2,4,16,128]{3,2,1,0:T(8,128)S(1)}, u32[]{:S(2)}, u32[]{:S(2)}) collective-permute-start(f32[2,4,16,128]{3,2,1,0:T(8,128)S(1)} %pad_maximum_fusion), channel_id=1, source_target_pairs={{0,63},{1,0},{2,1},{3,2},{4,3},{5,4},{6,5},{7,6},{8,7},{9,8},{10,9... | collective-permute-start | bytes 196616 | tf_op jit(solution)/shard_map/ppermute | solution.py:38
  17.5 9.5 %collective-permute-start = (f32[2,2,16,128]{3,2,1,0:T(8,128)S(1)}, f32[2,2,16,128]{3,2,1,0:T(8,128)S(1)}, u32[]{:S(2)}, u32[]{:S(2)}) collective-permute-start(f32[2,2,16,128]{3,2,1,0:T(8,128)S(1)} %get-tuple-element.38), channel_id=1, source_target_pairs={{0,2},{1,3},{2,4},{3,5},{4,6},{5,7},{6,8},{7,9},{8,10},{9,11},{10,... | collective-permute-start | bytes 98312 | tf_op jit(solution)/shard_map/ppermute | solution.py:37
  19.4 9.1 %collective-permute-start.3 = (f32[2,2,16,128]{3,2,1,0:T(8,128)S(1)}, f32[2,2,16,128]{3,2,1,0:T(8,128)S(1)}, u32[]{:S(2)}, u32[]{:S(2)}) collective-permute-start(f32[2,2,16,128]{3,2,1,0:T(8,128)S(1)} %get-tuple-element.37), channel_id=1, source_target_pairs={{0,62},{1,63},{2,0},{3,1},{4,2},{5,3},{6,4},{7,5},{8,6},{9,7},{10,... | collective-permute-start | bytes 98312 | tf_op jit(solution)/shard_map/ppermute | solution.py:38
  31.3 11.0 %copy-start.1 = (f32[8,1,16,16,128]{4,3,2,1,0:T(8,128)}, f32[8,1,16,16,128]{4,3,2,1,0:T(8,128)S(1)}, u32[]{:S(2)}) copy-start(f32[8,1,16,16,128]{4,3,2,1,0:T(8,128)S(1)} %get-tuple-element.36.mob_ref) | copy-start | bytes 3145732
  31.3 97.3 %copy-start = (f32[8,1,16,16,128]{4,3,2,1,0:T(8,128)}, f32[8,1,16,16,128]{4,3,2,1,0:T(8,128)S(1)}, u32[]{:S(2)}) copy-start(f32[8,1,16,16,128]{4,3,2,1,0:T(8,128)S(1)} %get-tuple-element.34.mob_ref) | copy-start | bytes 3145732
  110.0 19.8 %collective-permute-start.5 = (f32[8,4,16,128]{3,2,1,0:T(8,128)}, f32[8,4,16,128]{3,2,1,0:T(8,128)S(1)}, u32[]{:S(2)}, u32[]{:S(2)}) collective-permute-start(f32[8,4,16,128]{3,2,1,0:T(8,128)} %bitcast.15), channel_id=1, source_target_pairs={{0,1},{1,2},{2,3},{3,4},{4,5},{5,6},{6,7},{7,8},{8,9},{9,10},{10,1... | collective-permute-start | bytes 786440 | tf_op jit(solution)/shard_map/ppermute | solution.py:37
  111.9 18.9 %collective-permute-start.6 = (f32[8,4,16,128]{3,2,1,0:T(8,128)}, f32[8,4,16,128]{3,2,1,0:T(8,128)S(1)}, u32[]{:S(2)}, u32[]{:S(2)}) collective-permute-start(f32[8,4,16,128]{3,2,1,0:T(8,128)} %bitcast.16), channel_id=1, source_target_pairs={{0,63},{1,0},{2,1},{3,2},{4,3},{5,4},{6,5},{7,6},{8,7},{9,8},{10,9... | collective-permute-start | bytes 786440 | tf_op jit(solution)/shard_map/ppermute | solution.py:38
  119.2 10.6 %collective-permute-start.4 = (f32[8,2,16,128]{3,2,1,0:T(8,128)S(1)}, f32[8,2,16,128]{3,2,1,0:T(8,128)S(1)}, u32[]{:S(2)}, u32[]{:S(2)}) collective-permute-start(f32[8,2,16,128]{3,2,1,0:T(8,128)S(1)} %get-tuple-element.30), channel_id=1, source_target_pairs={{0,2},{1,3},{2,4},{3,5},{4,6},{5,7},{6,8},{7,9},{8,10},{9,11},{10,... | collective-permute-start | bytes 393224 | tf_op jit(solution)/shard_map/ppermute | solution.py:37
  121.1 10.0 %collective-permute-start.7 = (f32[8,2,16,128]{3,2,1,0:T(8,128)S(1)}, f32[8,2,16,128]{3,2,1,0:T(8,128)S(1)}, u32[]{:S(2)}, u32[]{:S(2)}) collective-permute-start(f32[8,2,16,128]{3,2,1,0:T(8,128)S(1)} %get-tuple-element.29), channel_id=1, source_target_pairs={{0,62},{1,63},{2,0},{3,1},{4,2},{5,3},{6,4},{7,5},{8,6},{9,7},{10,... | collective-permute-start | bytes 393224 | tf_op jit(solution)/shard_map/ppermute | solution.py:38
  131.2 1.0 copy-start.2

commit v2 on v1

--- a/solution.py
+++ b/solution.py
@@ -172,16 +172,29 @@
         out_rates_ref = None
     node = sel_ref[pl.program_id(0)]
     count = rates_ref.shape[0]
-    dt_tau = time_step * coef_ref[node, count]
-    weights = [coef_ref[node, j] for j in range(count)]
+    if not first:
+        dt_tau = time_step * coef_ref[node, count]
+        weights = [coef_ref[node, j] for j in range(count)]
+    if first:
+        count = mob_ref.shape[0]
+        weights = [coef_ref[node, j] for j in range(count)]
+        dt_tau = time_step * coef_ref[node, count]
     goal_planes = goal_sc.shape[1]
     off_goal = depth - (halo - 1)
 
     def goal_body(z, carry):
-        acc = rates_ref[0, :, z] * weights[0]
-        for j in range(1, count):
-            acc = acc + rates_ref[j, :, z] * weights[j]
-        goal_sc[:, z] = start_ref[:, z + off_goal] + time_step * acc - dt_tau * rates_ref[node, :, z]
+        if first:
+            bracket = rates_ref[:, z]
+            mix = -mob_ref[0, :, z + off_goal] * weights[0]
+            for j in range(1, count):
+                mix = mix + -mob_ref[j, :, z + off_goal] * weights[j]
+            own = -mob_ref[node, :, z + off_goal] * bracket
+            goal_sc[:, z] = start_ref[:, z + off_goal] + time_step * (mix * bracket) - dt_tau * own
+        else:
+            acc = rates_ref[0, :, z] * weights[0]
+            for j in range(1, count):
+                acc = acc + rates_ref[j, :, z] * weights[j]
+            goal_sc[:, z] = start_ref[:, z + off_goal] + time_step * acc - dt_tau * rates_ref[node, :, z]
         return carry
 
     lax.fori_loop(0, goal_planes, goal_body, 0)
@@ -195,8 +208,9 @@
         if index == 0 and first:
             def body(z, carry, target=target, off_fac=off_fac):
                 f = fac_ref[0, :, z + off_fac]
+                inv = 1.0 / (1.0 + 6.0 * f)
                 target_view = target.at[0] if target is out_ref else target
-                target_view[:, z] = (goal_sc[:, z] + f * state_ref[:, z]) / (1.0 + 6.0 * f)
+                target_view[:, z] = (goal_sc[:, z] + f * state_ref[:, z]) * inv
                 return carry
         else:
             def body(z, carry, target=target, off_fac=off_fac, source=source, index=index):
@@ -207,7 +221,8 @@
                 f = fac_ref[0, :, z + off_fac]
                 center = src[:, z + 1]
                 near = plane_near(src[:, z], center, src[:, z + 2])
-                value = (goal_sc[:, z + index] + f * (near - plane_drive(center))) / (1.0 + 6.0 * f)
+                inv = 1.0 / (1.0 + 6.0 * f)
+                value = (goal_sc[:, z + index] + f * (near - plane_drive(center))) * inv
                 target_view = target.at[0] if target is out_ref else target
                 target_view[:, z] = value
                 return carry
@@ -221,7 +236,7 @@
 
         def rate_body(z, carry):
             src = out_ref.at[0]
-            mob = mob_ref[0, :, z + off_mob]
+            mob = mob_ref[node if first else 0, :, z + off_mob]
             center = src[:, z + 1]
             near = plane_near(src[:, z], center, src[:, z + 2])
             out_rates_ref[0, :, z] = -mob * (plane_drive(center) - (near - 6.0 * center))
@@ -231,7 +246,7 @@
 
 
 def sweep_call(sel, coef, state, rates, start, factor, mobility, halo, depth, first, with_rates):
-    count, order, goal_planes, rows, lanes = rates.shape
+    order, goal_planes, rows, lanes = rates.shape[-4:]
     picks = sel.shape[0]
     out_planes = goal_planes - 2 * (JACOBI - 1)
     whole5 = lambda i, sel_ref: (0, 0, 0, 0, 0)
@@ -245,10 +260,10 @@
     in_specs = [
         pl.BlockSpec(memory_space=pltpu.SMEM),
         state_spec,
-        pl.BlockSpec(rates.shape, whole5),
+        pl.BlockSpec(rates.shape, whole4 if first else whole5),
         pl.BlockSpec(start.shape, whole4),
         pl.BlockSpec((1,) + factor.shape[1:], per_node),
-        pl.BlockSpec((1,) + mobility.shape[1:], per_node),
+        pl.BlockSpec(mobility.shape, whole5) if first else pl.BlockSpec((1,) + mobility.shape[1:], per_node),
     ]
     out_shape = [jax.ShapeDtypeStruct((picks, order, out_planes, rows, lanes), jnp.float32)]
     out_specs = [pl.BlockSpec((1, order, out_planes, rows, lanes), per_out)]
@@ -300,8 +315,7 @@
         moments = (step_index + times) * time_step
         mobility = heat_mobility(peak_wide[None], moments[:, None, None, None])[:, None]
         factor = time_step * taus * mobility
-        bracket, pull = prep_call(start)
-        rates = -trim(mobility, 1) * bracket[None]
+        rates, pull = prep_call(start)
         halo = depth
         states = pull
         for sweep_index in range(SWEEPS):

time: 209 us -> 189 us (0.904)
  other arithmetic: 17.4 us -> 7.3 us
  Pallas kernels: 140 us -> 132 us
    mul x5 -> x0, other arithmetic: 13 us -> none  [the longest x4 10.2 us: on_device(): rates = -trim(mobility, 1) * bracket[None]]
    pallas_call x6, Pallas kernels: 132 us -> 123 us  [sweep_call(): pl.pallas_call(kernel, out_shape=tuple(out_shape), grid_spec=pltpu.Prefet...]
    exp x0 -> x1, other arithmetic: none -> 3.11 us  [heat_mobility(): return jnp.exp(activation * (1.0 - 1.0 / theta))]
  transfers between devices with their start and end apart: 8 -> 8, of which waited for: 3 -> 2; matrix products, arithmetic and copies ran while one was open for 1% -> 2% of each run, Pallas kernels for 0% -> 0%
where the time goes in v2:
time: 189 us; the launch traced here: 188 us
  Pallas kernels  132 us (70%)
  starting transfers between devices  41.5 us (22%)
  other arithmetic  7.3 us (4%)
  local copies, waits for them, and re-layouts  5.06 us (3%)
  waiting for transfers between devices  2.33 us (1%)
    pallas_call x6, Pallas kernels, sweep_call(): pl.pallas_call(kernel, out_shape=tuple(out_shape), grid_spec=pltpu.Prefet...  123 us
    ppermute x4, starting transfers between devices, gather_halo(): lax.ppermute(lax.slice_in_dim(block, 0, take, axis=dim), axis, down)  33.8 us
    pallas_call x2, Pallas kernels, prep_call(): pl.pallas_call(prep_kernel, out_shape=(shape, shape), in_specs=[pl.BlockS...  8.05 us
    ppermute x4, starting transfers between devices, gather_halo(): lax.ppermute(lax.slice_in_dim(block, size - take, size, axis=dim), axis, up)  7.65 us
  transfers between devices with their start and end apart: 8, of which 2 were waited for; matrix products, arithmetic and copies ran while one was open for 2% of the time, Pallas kernels for 0%

profile of v2, /device:TPU:24, one launch (start us, length us, event | category | flops | bytes accessed | tf_op | source)
XLA Modules:
  0.0 187.8 jit_solution(17244986473205091633)
XLA Ops:
  0.0 0.8 convert_bitcast_fusion
  0.8 0.8 pad_maximum_fusion
  1.5 1.9 %collective-permute-start.1 = (f32[2,4,16,128]{3,2,1,0:T(8,128)S(1)}, f32[2,4,16,128]{3,2,1,0:T(8,128)S(1)}, u32[]{:S(2)}, u32[]{:S(2)}) collective-permute-start(f32[2,4,16,128]{3,2,1,0:T(8,128)S(1)} %pad_maximum_fusion), channel_id=1, source_target_pairs={{0,1},{1,2},{2,3},{3,4},{4,5},{5,6},{6,7},{7,8},{8,9},{9,10},{10,1... | collective-permute-start | bytes 196616 | tf_op jit(solution)/shard_map/ppermute | solution.py:37
  3.4 13.3 %collective-permute-start.2 = (f32[2,4,16,128]{3,2,1,0:T(8,128)S(1)}, f32[2,4,16,128]{3,2,1,0:T(8,128)S(1)}, u32[]{:S(2)}, u32[]{:S(2)}) collective-permute-start(f32[2,4,16,128]{3,2,1,0:T(8,128)S(1)} %pad_maximum_fusion), channel_id=1, source_target_pairs={{0,63},{1,0},{2,1},{3,2},{4,3},{5,4},{6,5},{7,6},{8,7},{9,8},{10,9... | collective-permute-start | bytes 196616 | tf_op jit(solution)/shard_map/ppermute | solution.py:38
  16.8 0.7 fusion.2
  17.5 1.9 %collective-permute-start = (f32[2,2,16,128]{3,2,1,0:T(8,128)S(1)}, f32[2,2,16,128]{3,2,1,0:T(8,128)S(1)}, u32[]{:S(2)}, u32[]{:S(2)}) collective-permute-start(f32[2,2,16,128]{3,2,1,0:T(8,128)S(1)} %get-tuple-element.38), channel_id=1, source_target_pairs={{0,2},{1,3},{2,4},{3,5},{4,6},{5,7},{6,8},{7,9},{8,10},{9,11},{10,... | collective-permute-start | bytes 98312 | tf_op jit(solution)/shard_map/ppermute | solution.py:37
  19.4 7.5 %collective-permute-start.3 = (f32[2,2,16,128]{3,2,1,0:T(8,128)S(1)}, f32[2,2,16,128]{3,2,1,0:T(8,128)S(1)}, u32[]{:S(2)}, u32[]{:S(2)}) collective-permute-start(f32[2,2,16,128]{3,2,1,0:T(8,128)S(1)} %get-tuple-element.37), channel_id=1, source_target_pairs={{0,62},{1,63},{2,0},{3,1},{4,2},{5,3},{6,4},{7,5},{8,6},{9,7},{10,... | collective-permute-start | bytes 98312 | tf_op jit(solution)/shard_map/ppermute | solution.py:38
  27.0 0.0 collective-permute-done
  27.0 0.8 constant_dynamic-update-slice_fusion.2
  27.8 0.7 collective-permute-done.3
  28.6 1.1 compare_convert_fusion.start_ref
  29.7 4.0 %shard_map.46 = (f32[8,14,16,128]{3,2,1,0:T(8,128)}, f32[8,14,16,128]{3,2,1,0:T(8,128)}) custom-call(f32[8,16,16,128]{3,2,1,0:T(8,128)} %compare_convert_fusion.start_ref), custom_call_target="tpu_custom_call" | custom-call | tf_op jit(solution)/shard_map/pallas_call | solution.py:156
  33.7 3.1 %multiply_exponential_fusion = (f32[8,1,16,16,128]{4,3,2,1,0:T(8,128)}, f32[8,1,16,16,128]{4,3,2,1,0:T(8,128)}, f32[8,1,16,16,128]{4,3,2,1,0:T(8,128)}, f32[8,1,16,16,128]{4,3,2,1,0:T(8,128)}) fusion(f32[8]{0:T(128)} %constant.48, f32[16,16,128]{2,1,0:T(8,128)S(1)} %get-tuple-element.31, f32[8]{0:T(128)} %constant.36, f32[8]{0:T(128)} %constant.41), kind=kLoop, calls=%fused_computation | loop fusion | flops 3145728 | bytes 4325472 | tf_op jit(solution)/shard_map/exp | solution.py:116
  36.8 0.5 iota.17.sel_ref
  37.3 27.6 %shard_map.47 = (f32[8,8,12,16,128]{4,3,2,1,0:T(8,128)}, f32[8,8,10,16,128]{4,3,2,1,0:T(8,128)}) custom-call(s32[8]{0:T(128)} %iota.17.sel_ref, f32[8,9]{1,0:T(8,128)} %constant.33.clone.coef_ref, f32[8,14,16,128]{3,2,1,0:T(8,128)} %get-tuple-element.17.state_ref, f32[8,14,16,128]{3,2,1,0:T(8,128)} %get-tuple-element.18.rates_ref, ...), custom_call_target="tpu_custom_call" | custom-call | tf_op jit(solution)/shard_map/pallas_call | solution.py:278
  64.9 0.5 iota.16.sel_ref
  65.4 29.7 %shard_map.48 = (f32[8,8,8,16,128]{4,3,2,1,0:T(8,128)}, f32[8,8,6,16,128]{4,3,2,1,0:T(8,128)}) custom-call(s32[8]{0:T(128)} %iota.16.sel_ref, f32[8,9]{1,0:T(8,128)} %constant.33.clone.coef_ref, f32[8,8,12,16,128]{4,3,2,1,0:T(8,128)} %get-tuple-element.19.state_ref, f32[8,8,10,16,128]{4,3,2,1,0:T(8,128)} %get-tuple-element.20.rates_ref, ...), custom_call_target="tpu_custom_call" | custom-call | tf_op jit(solution)/shard_map/pallas_call | solution.py:278
  95.1 4.5 %shard_map.49 = f32[1,8,4,16,128]{4,3,2,1,0:T(8,128)} custom-call(s32[1]{0:T(128)} %constant.10.clone.1.sel_ref, f32[8,9]{1,0:T(8,128)} %constant.33.clone.coef_ref, f32[8,8,8,16,128]{4,3,2,1,0:T(8,128)} %get-tuple-element.21.state_ref, f32[8,8,6,16,128]{4,3,2,1,0:T(8,128)} %get-tuple-element.22.rates_ref, f32[8,16,16,128]{3,2,1,0:T(8,128)} %compare_convert_fusion.start_ref, ...), custom_call_target="tpu_custom_call" | custom-call | tf_op jit(solution)/shard_map/pallas_call | solution.py:278
  99.6 1.9 %collective-permute-start.5 = (f32[8,4,16,128]{3,2,1,0:T(8,128)}, f32[8,4,16,128]{3,2,1,0:T(8,128)S(1)}, u32[]{:S(2)}, u32[]{:S(2)}) collective-permute-start(f32[8,4,16,128]{3,2,1,0:T(8,128)} %bitcast.10), channel_id=1, source_target_pairs={{0,1},{1,2},{2,3},{3,4},{4,5},{5,6},{6,7},{7,8},{8,9},{9,10},{10,1... | collective-permute-start | bytes 786440 | tf_op jit(solution)/shard_map/ppermute | solution.py:37
  101.5 1.0 fusion.3
  102.5 1.9 %collective-permute-start.4 = (f32[8,2,16,128]{3,2,1,0:T(8,128)S(1)}, f32[8,2,16,128]{3,2,1,0:T(8,128)S(1)}, u32[]{:S(2)}, u32[]{:S(2)}) collective-permute-start(f32[8,2,16,128]{3,2,1,0:T(8,128)S(1)} %get-tuple-element.30), channel_id=1, source_target_pairs={{0,2},{1,3},{2,4},{3,5},{4,6},{5,7},{6,8},{7,9},{8,10},{9,11},{10,... | collective-permute-start | bytes 393224 | tf_op jit(solution)/shard_map/ppermute | solution.py:37
  104.4 7.3 %collective-permute-start.6 = (f32[8,4,16,128]{3,2,1,0:T(8,128)}, f32[8,4,16,128]{3,2,1,0:T(8,128)S(1)}, u32[]{:S(2)}, u32[]{:S(2)}) collective-permute-start(f32[8,4,16,128]{3,2,1,0:T(8,128)} %bitcast.12), channel_id=1, source_target_pairs={{0,63},{1,0},{2,1},{3,2},{4,3},{5,4},{6,5},{7,6},{8,7},{9,8},{10,9... | collective-permute-start | bytes 786440 | tf_op jit(solution)/shard_map/ppermute | solution.py:38
  111.7 5.7 %collective-permute-start.7 = (f32[8,2,16,128]{3,2,1,0:T(8,128)S(1)}, f32[8,2,16,128]{3,2,1,0:T(8,128)S(1)}, u32[]{:S(2)}, u32[]{:S(2)}) collective-permute-start(f32[8,2,16,128]{3,2,1,0:T(8,128)S(1)} %get-tuple-element.29), channel_id=1, source_target_pairs={{0,62},{1,63},{2,0},{3,1},{4,2},{5,3},{6,4},{7,5},{8,6},{9,7},{10,... | collective-permute-start | bytes 393224 | tf_op jit(solution)/shard_map/ppermute | solution.py:38
  117.5 1.0 constant_dynamic-update-slice_fusion.7
  118.5 1.5 collective-permute-done.7
  120.1 1.0 copy-done
  121.1 4.0 %shard_map.50 = (f32[8,14,16,128]{3,2,1,0:T(8,128)}, f32[8,14,16,128]{3,2,1,0:T(8,128)}) custom-call(f32[8,16,16,128]{3,2,1,0:T(8,128)} %copy-done), custom_call_target="tpu_custom_call" | custom-call | tf_op jit(solution)/shard_map/pallas_call | solution.py:156
  125.1 0.5 iota.15.sel_ref
  125.6 27.6 %shard_map.51 = (f32[8,8,12,16,128]{4,3,2,1,0:T(8,128)}, f32[8,8,10,16,128]{4,3,2,1,0:T(8,128)}) custom-call(s32[8]{0:T(128)} %iota.15.sel_ref, f32[8,9]{1,0:T(8,128)} %constant.33.clone.coef_ref, f32[8,14,16,128]{3,2,1,0:T(8,128)} %get-tuple-element.23.state_ref, f32[8,14,16,128]{3,2,1,0:T(8,128)} %get-tuple-element.24.rates_ref, ...), custom_call_target="tpu_custom_call" | custom-call | tf_op jit(solution)/shard_map/pallas_call | solution.py:278
  153.2 0.5 iota.14.sel_ref
  153.7 29.7 %shard_map.52 = (f32[8,8,8,16,128]{4,3,2,1,0:T(8,128)}, f32[8,8,6,16,128]{4,3,2,1,0:T(8,128)}) custom-call(s32[8]{0:T(128)} %iota.14.sel_ref, f32[8,9]{1,0:T(8,128)} %constant.33.clone.coef_ref, f32[8,8,12,16,128]{4,3,2,1,0:T(8,128)} %get-tuple-element.25.state_ref, f32[8,8,10,16,128]{4,3,2,1,0:T(8,128)} %get-tuple-element.26.rates_ref, ...), custom_call_target="tpu_custom_call" | custom-call | tf_op jit(solution)/shard_map/pallas_call | solution.py:278
  183.4 4.5 %shard_map.53 = f32[1,8,4,16,128]{4,3,2,1,0:T(8,128)} custom-call(s32[1]{0:T(128)} %bitcast.sel_ref, f32[8,9]{1,0:T(8,128)} %constant.33.clone.coef_ref, f32[8,8,8,16,128]{4,3,2,1,0:T(8,128)} %get-tuple-element.27.state_ref, f32[8,8,6,16,128]{4,3,2,1,0:T(8,128)} %get-tuple-element.28.rates_ref, f32[8,16,16,128]{3,2,1,0:T(8,128)} %copy-done, ...), custom_call_target="tpu_custom_call" | custom-call | tf_op jit(solution)/shard_map/pallas_call | solution.py:278
  (16 shorter events, 0.1 us)
Async XLA Ops:
  1.5 25.5 %collective-permute-start.1 = (f32[2,4,16,128]{3,2,1,0:T(8,128)S(1)}, f32[2,4,16,128]{3,2,1,0:T(8,128)S(1)}, u32[]{:S(2)}, u32[]{:S(2)}) collective-permute-start(f32[2,4,16,128]{3,2,1,0:T(8,128)S(1)} %pad_maximum_fusion), channel_id=1, source_target_pairs={{0,1},{1,2},{2,3},{3,4},{4,5},{5,6},{6,7},{7,8},{8,9},{9,10},{10,1... | collective-permute-start | bytes 196616 | tf_op jit(solution)/shard_map/ppermute | solution.py:37
  3.4 24.4 %collective-permute-start.2 = (f32[2,4,16,128]{3,2,1,0:T(8,128)S(1)}, f32[2,4,16,128]{3,2,1,0:T(8,128)S(1)}, u32[]{:S(2)}, u32[]{:S(2)}) collective-permute-start(f32[2,4,16,128]{3,2,1,0:T(8,128)S(1)} %pad_maximum_fusion), channel_id=1, source_target_pairs={{0,63},{1,0},{2,1},{3,2},{4,3},{5,4},{6,5},{7,6},{8,7},{9,8},{10,9... | collective-permute-start | bytes 196616 | tf_op jit(solution)/shard_map/ppermute | solution.py:38
  17.5 9.5 %collective-permute-start = (f32[2,2,16,128]{3,2,1,0:T(8,128)S(1)}, f32[2,2,16,128]{3,2,1,0:T(8,128)S(1)}, u32[]{:S(2)}, u32[]{:S(2)}) collective-permute-start(f32[2,2,16,128]{3,2,1,0:T(8,128)S(1)} %get-tuple-element.38), channel_id=1, source_target_pairs={{0,2},{1,3},{2,4},{3,5},{4,6},{5,7},{6,8},{7,9},{8,10},{9,11},{10,... | collective-permute-start | bytes 98312 | tf_op jit(solution)/shard_map/ppermute | solution.py:37
  19.4 9.1 %collective-permute-start.3 = (f32[2,2,16,128]{3,2,1,0:T(8,128)S(1)}, f32[2,2,16,128]{3,2,1,0:T(8,128)S(1)}, u32[]{:S(2)}, u32[]{:S(2)}) collective-permute-start(f32[2,2,16,128]{3,2,1,0:T(8,128)S(1)} %get-tuple-element.37), channel_id=1, source_target_pairs={{0,62},{1,63},{2,0},{3,1},{4,2},{5,3},{6,4},{7,5},{8,6},{9,7},{10,... | collective-permute-start | bytes 98312 | tf_op jit(solution)/shard_map/ppermute | solution.py:38
  99.6 17.9 %collective-permute-start.5 = (f32[8,4,16,128]{3,2,1,0:T(8,128)}, f32[8,4,16,128]{3,2,1,0:T(8,128)S(1)}, u32[]{:S(2)}, u32[]{:S(2)}) collective-permute-start(f32[8,4,16,128]{3,2,1,0:T(8,128)} %bitcast.10), channel_id=1, source_target_pairs={{0,1},{1,2},{2,3},{3,4},{4,5},{5,6},{6,7},{7,8},{8,9},{9,10},{10,1... | collective-permute-start | bytes 786440 | tf_op jit(solution)/shard_map/ppermute | solution.py:37
  102.5 14.9 %collective-permute-start.4 = (f32[8,2,16,128]{3,2,1,0:T(8,128)S(1)}, f32[8,2,16,128]{3,2,1,0:T(8,128)S(1)}, u32[]{:S(2)}, u32[]{:S(2)}) collective-permute-start(f32[8,2,16,128]{3,2,1,0:T(8,128)S(1)} %get-tuple-element.30), channel_id=1, source_target_pairs={{0,2},{1,3},{2,4},{3,5},{4,6},{5,7},{6,8},{7,9},{8,10},{9,11},{10,... | collective-permute-start | bytes 393224 | tf_op jit(solution)/shard_map/ppermute | solution.py:37
  104.4 14.0 %collective-permute-start.6 = (f32[8,4,16,128]{3,2,1,0:T(8,128)}, f32[8,4,16,128]{3,2,1,0:T(8,128)S(1)}, u32[]{:S(2)}, u32[]{:S(2)}) collective-permute-start(f32[8,4,16,128]{3,2,1,0:T(8,128)} %bitcast.12), channel_id=1, source_target_pairs={{0,63},{1,0},{2,1},{3,2},{4,3},{5,4},{6,5},{7,6},{8,7},{9,8},{10,9... | collective-permute-start | bytes 786440 | tf_op jit(solution)/shard_map/ppermute | solution.py:38
  111.7 8.4 %collective-permute-start.7 = (f32[8,2,16,128]{3,2,1,0:T(8,128)S(1)}, f32[8,2,16,128]{3,2,1,0:T(8,128)S(1)}, u32[]{:S(2)}, u32[]{:S(2)}) collective-permute-start(f32[8,2,16,128]{3,2,1,0:T(8,128)S(1)} %get-tuple-element.29), channel_id=1, source_target_pairs={{0,62},{1,63},{2,0},{3,1},{4,2},{5,3},{6,4},{7,5},{8,6},{9,7},{10,... | collective-permute-start | bytes 393224 | tf_op jit(solution)/shard_map/ppermute | solution.py:38
  120.1 1.0 copy-start

commit v3 on v2

--- a/solution.py
+++ b/solution.py
@@ -135,7 +135,7 @@
 def plane_drive(field):
     squares = field * field
     total = jnp.sum(squares, axis=0, keepdims=True)
-    return -field + squares * field + 2.0 * cross_coef * field * (total - squares)
+    return field * ((2.0 * cross_coef * total - 1.0) - (2.0 * cross_coef - 1.0) * squares)
 
 
 def prep_kernel(start_ref, bracket_ref, pull_ref):
@@ -147,7 +147,7 @@
         pull_ref[:, z] = near - push
         return carry
 
-    lax.fori_loop(0, bracket_ref.shape[1], body, 0)
+    lax.fori_loop(0, bracket_ref.shape[1], body, 0, unroll=True)
 
 
 def prep_call(start):
@@ -197,7 +197,7 @@
             goal_sc[:, z] = start_ref[:, z + off_goal] + time_step * acc - dt_tau * rates_ref[node, :, z]
         return carry
 
-    lax.fori_loop(0, goal_planes, goal_body, 0)
+    lax.fori_loop(0, goal_planes, goal_body, 0, unroll=True)
 
     source = None
     for index in range(jacobi):
@@ -227,7 +227,7 @@
                 target_view[:, z] = value
                 return carry
 
-        lax.fori_loop(0, planes, body, 0)
+        lax.fori_loop(0, planes, body, 0, unroll=True)
         source = target.at[0] if target is out_ref else target
 
     if with_rates:
@@ -242,7 +242,7 @@
             out_rates_ref[0, :, z] = -mob * (plane_drive(center) - (near - 6.0 * center))
             return carry
 
-        lax.fori_loop(0, out_rates_ref.shape[2], rate_body, 0)
+        lax.fori_loop(0, out_rates_ref.shape[2], rate_body, 0, unroll=True)
 
 
 def sweep_call(sel, coef, state, rates, start, factor, mobility, halo, depth, first, with_rates):

time: 189 us -> 133 us (0.70)
  Pallas kernels: 132 us -> 75 us
    pallas_call x6, Pallas kernels: 123 us -> 68.6 us  [sweep_call(): pl.pallas_call(kernel, out_shape=tuple(out_shape), grid_spec=pltpu.Prefet...]
  transfers between devices with their start and end apart: 8 -> 8, of which waited for: 2 -> 2; matrix products, arithmetic and copies ran while one was open for 2% -> 3% of each run, Pallas kernels for 0% -> 0%
where the time goes in v3:
time: 133 us; the launch traced here: 131 us
  Pallas kernels  75 us (56%)
  starting transfers between devices  41.5 us (31%)
  other arithmetic  7.3 us (5%)
  local copies, waits for them, and re-layouts  5.06 us (4%)
  waiting for transfers between devices  2.33 us (2%)
    pallas_call x6, Pallas kernels, sweep_call(): pl.pallas_call(kernel, out_shape=tuple(out_shape), grid_spec=pltpu.Prefet...  68.6 us
    ppermute x4, starting transfers between devices, gather_halo(): lax.ppermute(lax.slice_in_dim(block, 0, take, axis=dim), axis, down)  33.8 us
    ppermute x4, starting transfers between devices, gather_halo(): lax.ppermute(lax.slice_in_dim(block, size - take, size, axis=dim), axis, up)  7.65 us
    pallas_call x2, Pallas kernels, prep_call(): pl.pallas_call(prep_kernel, out_shape=(shape, shape), in_specs=[pl.BlockS...  6.4 us
    exp x1, other arithmetic, heat_mobility(): return jnp.exp(activation * (1.0 - 1.0 / theta))  3.11 us
  transfers between devices with their start and end apart: 8, of which 2 were waited for; matrix products, arithmetic and copies ran while one was open for 3% of the time, Pallas kernels for 0%

profile of v3, /device:TPU:24, one launch (start us, length us, event | category | flops | bytes accessed | tf_op | source)
XLA Modules:
  0.0 131.3 jit_solution(1036045927018200373)
XLA Ops:
  0.0 0.8 convert_bitcast_fusion
  0.8 0.8 pad_maximum_fusion
  1.5 1.9 %collective-permute-start.1 = (f32[2,4,16,128]{3,2,1,0:T(8,128)S(1)}, f32[2,4,16,128]{3,2,1,0:T(8,128)S(1)}, u32[]{:S(2)}, u32[]{:S(2)}) collective-permute-start(f32[2,4,16,128]{3,2,1,0:T(8,128)S(1)} %pad_maximum_fusion), channel_id=1, source_target_pairs={{0,1},{1,2},{2,3},{3,4},{4,5},{5,6},{6,7},{7,8},{8,9},{9,10},{10,1... | collective-permute-start | bytes 196616 | tf_op jit(solution)/shard_map/ppermute | solution.py:37
  3.4 13.3 %collective-permute-start.2 = (f32[2,4,16,128]{3,2,1,0:T(8,128)S(1)}, f32[2,4,16,128]{3,2,1,0:T(8,128)S(1)}, u32[]{:S(2)}, u32[]{:S(2)}) collective-permute-start(f32[2,4,16,128]{3,2,1,0:T(8,128)S(1)} %pad_maximum_fusion), channel_id=1, source_target_pairs={{0,63},{1,0},{2,1},{3,2},{4,3},{5,4},{6,5},{7,6},{8,7},{9,8},{10,9... | collective-permute-start | bytes 196616 | tf_op jit(solution)/shard_map/ppermute | solution.py:38
  16.8 0.7 fusion.2
  17.5 1.9 %collective-permute-start = (f32[2,2,16,128]{3,2,1,0:T(8,128)S(1)}, f32[2,2,16,128]{3,2,1,0:T(8,128)S(1)}, u32[]{:S(2)}, u32[]{:S(2)}) collective-permute-start(f32[2,2,16,128]{3,2,1,0:T(8,128)S(1)} %get-tuple-element.38), channel_id=1, source_target_pairs={{0,2},{1,3},{2,4},{3,5},{4,6},{5,7},{6,8},{7,9},{8,10},{9,11},{10,... | collective-permute-start | bytes 98312 | tf_op jit(solution)/shard_map/ppermute | solution.py:37
  19.4 7.5 %collective-permute-start.3 = (f32[2,2,16,128]{3,2,1,0:T(8,128)S(1)}, f32[2,2,16,128]{3,2,1,0:T(8,128)S(1)}, u32[]{:S(2)}, u32[]{:S(2)}) collective-permute-start(f32[2,2,16,128]{3,2,1,0:T(8,128)S(1)} %get-tuple-element.37), channel_id=1, source_target_pairs={{0,62},{1,63},{2,0},{3,1},{4,2},{5,3},{6,4},{7,5},{8,6},{9,7},{10,... | collective-permute-start | bytes 98312 | tf_op jit(solution)/shard_map/ppermute | solution.py:38
  27.0 0.0 collective-permute-done
  27.0 0.8 constant_dynamic-update-slice_fusion.2
  27.8 0.7 collective-permute-done.3
  28.6 1.1 compare_convert_fusion.start_ref
  29.7 3.2 %shard_map.46 = (f32[8,14,16,128]{3,2,1,0:T(8,128)}, f32[8,14,16,128]{3,2,1,0:T(8,128)}) custom-call(f32[8,16,16,128]{3,2,1,0:T(8,128)} %compare_convert_fusion.start_ref), custom_call_target="tpu_custom_call" | custom-call | tf_op jit(solution)/shard_map/pallas_call | solution.py:156
  32.9 3.1 %multiply_exponential_fusion = (f32[8,1,16,16,128]{4,3,2,1,0:T(8,128)}, f32[8,1,16,16,128]{4,3,2,1,0:T(8,128)}, f32[8,1,16,16,128]{4,3,2,1,0:T(8,128)}, f32[8,1,16,16,128]{4,3,2,1,0:T(8,128)}) fusion(f32[8]{0:T(128)} %constant.48, f32[16,16,128]{2,1,0:T(8,128)S(1)} %get-tuple-element.31, f32[8]{0:T(128)} %constant.36, f32[8]{0:T(128)} %constant.41), kind=kLoop, calls=%fused_computation | loop fusion | flops 3145728 | bytes 4325472 | tf_op jit(solution)/shard_map/exp | solution.py:116
  36.0 0.5 iota.17.sel_ref
  36.5 14.3 %shard_map.47 = (f32[8,8,12,16,128]{4,3,2,1,0:T(8,128)}, f32[8,8,10,16,128]{4,3,2,1,0:T(8,128)}) custom-call(s32[8]{0:T(128)} %iota.17.sel_ref, f32[8,9]{1,0:T(8,128)} %constant.33.clone.coef_ref, f32[8,14,16,128]{3,2,1,0:T(8,128)} %get-tuple-element.17.state_ref, f32[8,14,16,128]{3,2,1,0:T(8,128)} %get-tuple-element.18.rates_ref, ...), custom_call_target="tpu_custom_call" | custom-call | tf_op jit(solution)/shard_map/pallas_call | solution.py:278
  50.8 0.5 iota.16.sel_ref
  51.3 16.3 %shard_map.48 = (f32[8,8,8,16,128]{4,3,2,1,0:T(8,128)}, f32[8,8,6,16,128]{4,3,2,1,0:T(8,128)}) custom-call(s32[8]{0:T(128)} %iota.16.sel_ref, f32[8,9]{1,0:T(8,128)} %constant.33.clone.coef_ref, f32[8,8,12,16,128]{4,3,2,1,0:T(8,128)} %get-tuple-element.19.state_ref, f32[8,8,10,16,128]{4,3,2,1,0:T(8,128)} %get-tuple-element.20.rates_ref, ...), custom_call_target="tpu_custom_call" | custom-call | tf_op jit(solution)/shard_map/pallas_call | solution.py:278
  67.6 3.7 %shard_map.49 = f32[1,8,4,16,128]{4,3,2,1,0:T(8,128)} custom-call(s32[1]{0:T(128)} %constant.10.clone.1.sel_ref, f32[8,9]{1,0:T(8,128)} %constant.33.clone.coef_ref, f32[8,8,8,16,128]{4,3,2,1,0:T(8,128)} %get-tuple-element.21.state_ref, f32[8,8,6,16,128]{4,3,2,1,0:T(8,128)} %get-tuple-element.22.rates_ref, f32[8,16,16,128]{3,2,1,0:T(8,128)} %compare_convert_fusion.start_ref, ...), custom_call_target="tpu_custom_call" | custom-call | tf_op jit(solution)/shard_map/pallas_call | solution.py:278
  71.3 1.9 %collective-permute-start.5 = (f32[8,4,16,128]{3,2,1,0:T(8,128)}, f32[8,4,16,128]{3,2,1,0:T(8,128)S(1)}, u32[]{:S(2)}, u32[]{:S(2)}) collective-permute-start(f32[8,4,16,128]{3,2,1,0:T(8,128)} %bitcast.10), channel_id=1, source_target_pairs={{0,1},{1,2},{2,3},{3,4},{4,5},{5,6},{6,7},{7,8},{8,9},{9,10},{10,1... | collective-permute-start | bytes 786440 | tf_op jit(solution)/shard_map/ppermute | solution.py:37
  73.2 1.0 fusion.3
  74.2 1.9 %collective-permute-start.4 = (f32[8,2,16,128]{3,2,1,0:T(8,128)S(1)}, f32[8,2,16,128]{3,2,1,0:T(8,128)S(1)}, u32[]{:S(2)}, u32[]{:S(2)}) collective-permute-start(f32[8,2,16,128]{3,2,1,0:T(8,128)S(1)} %get-tuple-element.30), channel_id=1, source_target_pairs={{0,2},{1,3},{2,4},{3,5},{4,6},{5,7},{6,8},{7,9},{8,10},{9,11},{10,... | collective-permute-start | bytes 393224 | tf_op jit(solution)/shard_map/ppermute | solution.py:37
  76.2 7.3 %collective-permute-start.6 = (f32[8,4,16,128]{3,2,1,0:T(8,128)}, f32[8,4,16,128]{3,2,1,0:T(8,128)S(1)}, u32[]{:S(2)}, u32[]{:S(2)}) collective-permute-start(f32[8,4,16,128]{3,2,1,0:T(8,128)} %bitcast.12), channel_id=1, source_target_pairs={{0,63},{1,0},{2,1},{3,2},{4,3},{5,4},{6,5},{7,6},{8,7},{9,8},{10,9... | collective-permute-start | bytes 786440 | tf_op jit(solution)/shard_map/ppermute | solution.py:38
  83.4 5.7 %collective-permute-start.7 = (f32[8,2,16,128]{3,2,1,0:T(8,128)S(1)}, f32[8,2,16,128]{3,2,1,0:T(8,128)S(1)}, u32[]{:S(2)}, u32[]{:S(2)}) collective-permute-start(f32[8,2,16,128]{3,2,1,0:T(8,128)S(1)} %get-tuple-element.29), channel_id=1, source_target_pairs={{0,62},{1,63},{2,0},{3,1},{4,2},{5,3},{6,4},{7,5},{8,6},{9,7},{10,... | collective-permute-start | bytes 393224 | tf_op jit(solution)/shard_map/ppermute | solution.py:38
  89.2 1.0 constant_dynamic-update-slice_fusion.7
  90.3 1.5 %collective-permute-done.7 = f32[8,2,16,128]{3,2,1,0:T(8,128)S(1)} collective-permute-done((f32[8,2,16,128]{3,2,1,0:T(8,128)S(1)}, f32[8,2,16,128]{3,2,1,0:T(8,128)S(1)}, u32[]{:S(2)}, u32[]{:S(2)}) %collective-permute-start.7) | collective-permute-done | bytes 131104 | tf_op jit(solution)/shard_map/ppermute | solution.py:38
  91.8 1.0 copy-done
  92.8 3.2 %shard_map.50 = (f32[8,14,16,128]{3,2,1,0:T(8,128)}, f32[8,14,16,128]{3,2,1,0:T(8,128)}) custom-call(f32[8,16,16,128]{3,2,1,0:T(8,128)} %copy-done), custom_call_target="tpu_custom_call" | custom-call | tf_op jit(solution)/shard_map/pallas_call | solution.py:156
  96.0 0.5 iota.15.sel_ref
  96.5 14.3 %shard_map.51 = (f32[8,8,12,16,128]{4,3,2,1,0:T(8,128)}, f32[8,8,10,16,128]{4,3,2,1,0:T(8,128)}) custom-call(s32[8]{0:T(128)} %iota.15.sel_ref, f32[8,9]{1,0:T(8,128)} %constant.33.clone.coef_ref, f32[8,14,16,128]{3,2,1,0:T(8,128)} %get-tuple-element.23.state_ref, f32[8,14,16,128]{3,2,1,0:T(8,128)} %get-tuple-element.24.rates_ref, ...), custom_call_target="tpu_custom_call" | custom-call | tf_op jit(solution)/shard_map/pallas_call | solution.py:278
  110.8 0.5 iota.14.sel_ref
  111.3 16.3 %shard_map.52 = (f32[8,8,8,16,128]{4,3,2,1,0:T(8,128)}, f32[8,8,6,16,128]{4,3,2,1,0:T(8,128)}) custom-call(s32[8]{0:T(128)} %iota.14.sel_ref, f32[8,9]{1,0:T(8,128)} %constant.33.clone.coef_ref, f32[8,8,12,16,128]{4,3,2,1,0:T(8,128)} %get-tuple-element.25.state_ref, f32[8,8,10,16,128]{4,3,2,1,0:T(8,128)} %get-tuple-element.26.rates_ref, ...), custom_call_target="tpu_custom_call" | custom-call | tf_op jit(solution)/shard_map/pallas_call | solution.py:278
  127.6 3.7 %shard_map.53 = f32[1,8,4,16,128]{4,3,2,1,0:T(8,128)} custom-call(s32[1]{0:T(128)} %bitcast.sel_ref, f32[8,9]{1,0:T(8,128)} %constant.33.clone.coef_ref, f32[8,8,8,16,128]{4,3,2,1,0:T(8,128)} %get-tuple-element.27.state_ref, f32[8,8,6,16,128]{4,3,2,1,0:T(8,128)} %get-tuple-element.28.rates_ref, f32[8,16,16,128]{3,2,1,0:T(8,128)} %copy-done, ...), custom_call_target="tpu_custom_call" | custom-call | tf_op jit(solution)/shard_map/pallas_call | solution.py:278
  (16 shorter events, 0.1 us)
Async XLA Ops:
  1.5 25.5 %collective-permute-start.1 = (f32[2,4,16,128]{3,2,1,0:T(8,128)S(1)}, f32[2,4,16,128]{3,2,1,0:T(8,128)S(1)}, u32[]{:S(2)}, u32[]{:S(2)}) collective-permute-start(f32[2,4,16,128]{3,2,1,0:T(8,128)S(1)} %pad_maximum_fusion), channel_id=1, source_target_pairs={{0,1},{1,2},{2,3},{3,4},{4,5},{5,6},{6,7},{7,8},{8,9},{9,10},{10,1... | collective-permute-start | bytes 196616 | tf_op jit(solution)/shard_map/ppermute | solution.py:37
  3.4 24.4 %collective-permute-start.2 = (f32[2,4,16,128]{3,2,1,0:T(8,128)S(1)}, f32[2,4,16,128]{3,2,1,0:T(8,128)S(1)}, u32[]{:S(2)}, u32[]{:S(2)}) collective-permute-start(f32[2,4,16,128]{3,2,1,0:T(8,128)S(1)} %pad_maximum_fusion), channel_id=1, source_target_pairs={{0,63},{1,0},{2,1},{3,2},{4,3},{5,4},{6,5},{7,6},{8,7},{9,8},{10,9... | collective-permute-start | bytes 196616 | tf_op jit(solution)/shard_map/ppermute | solution.py:38
  17.5 9.5 %collective-permute-start = (f32[2,2,16,128]{3,2,1,0:T(8,128)S(1)}, f32[2,2,16,128]{3,2,1,0:T(8,128)S(1)}, u32[]{:S(2)}, u32[]{:S(2)}) collective-permute-start(f32[2,2,16,128]{3,2,1,0:T(8,128)S(1)} %get-tuple-element.38), channel_id=1, source_target_pairs={{0,2},{1,3},{2,4},{3,5},{4,6},{5,7},{6,8},{7,9},{8,10},{9,11},{10,... | collective-permute-start | bytes 98312 | tf_op jit(solution)/shard_map/ppermute | solution.py:37
  19.4 9.1 %collective-permute-start.3 = (f32[2,2,16,128]{3,2,1,0:T(8,128)S(1)}, f32[2,2,16,128]{3,2,1,0:T(8,128)S(1)}, u32[]{:S(2)}, u32[]{:S(2)}) collective-permute-start(f32[2,2,16,128]{3,2,1,0:T(8,128)S(1)} %get-tuple-element.37), channel_id=1, source_target_pairs={{0,62},{1,63},{2,0},{3,1},{4,2},{5,3},{6,4},{7,5},{8,6},{9,7},{10,... | collective-permute-start | bytes 98312 | tf_op jit(solution)/shard_map/ppermute | solution.py:38
  71.3 17.9 %collective-permute-start.5 = (f32[8,4,16,128]{3,2,1,0:T(8,128)}, f32[8,4,16,128]{3,2,1,0:T(8,128)S(1)}, u32[]{:S(2)}, u32[]{:S(2)}) collective-permute-start(f32[8,4,16,128]{3,2,1,0:T(8,128)} %bitcast.10), channel_id=1, source_target_pairs={{0,1},{1,2},{2,3},{3,4},{4,5},{5,6},{6,7},{7,8},{8,9},{9,10},{10,1... | collective-permute-start | bytes 786440 | tf_op jit(solution)/shard_map/ppermute | solution.py:37
  74.2 14.9 %collective-permute-start.4 = (f32[8,2,16,128]{3,2,1,0:T(8,128)S(1)}, f32[8,2,16,128]{3,2,1,0:T(8,128)S(1)}, u32[]{:S(2)}, u32[]{:S(2)}) collective-permute-start(f32[8,2,16,128]{3,2,1,0:T(8,128)S(1)} %get-tuple-element.30), channel_id=1, source_target_pairs={{0,2},{1,3},{2,4},{3,5},{4,6},{5,7},{6,8},{7,9},{8,10},{9,11},{10,... | collective-permute-start | bytes 393224 | tf_op jit(solution)/shard_map/ppermute | solution.py:37
  76.2 14.0 %collective-permute-start.6 = (f32[8,4,16,128]{3,2,1,0:T(8,128)}, f32[8,4,16,128]{3,2,1,0:T(8,128)S(1)}, u32[]{:S(2)}, u32[]{:S(2)}) collective-permute-start(f32[8,4,16,128]{3,2,1,0:T(8,128)} %bitcast.12), channel_id=1, source_target_pairs={{0,63},{1,0},{2,1},{3,2},{4,3},{5,4},{6,5},{7,6},{8,7},{9,8},{10,9... | collective-permute-start | bytes 786440 | tf_op jit(solution)/shard_map/ppermute | solution.py:38
  83.4 8.4 %collective-permute-start.7 = (f32[8,2,16,128]{3,2,1,0:T(8,128)S(1)}, f32[8,2,16,128]{3,2,1,0:T(8,128)S(1)}, u32[]{:S(2)}, u32[]{:S(2)}) collective-permute-start(f32[8,2,16,128]{3,2,1,0:T(8,128)S(1)} %get-tuple-element.29), channel_id=1, source_target_pairs={{0,62},{1,63},{2,0},{3,1},{4,2},{5,3},{6,4},{7,5},{8,6},{9,7},{10,... | collective-permute-start | bytes 393224 | tf_op jit(solution)/shard_map/ppermute | solution.py:38
  91.8 1.0 copy-start

commit v4 on v3

--- a/solution.py
+++ b/solution.py
@@ -127,9 +127,14 @@
 
 
 def plane_near(below, center, above):
+    even = center[:, 0:1]
+    odd = center[:, 1:2]
+    rows = center.shape[2]
+    y_next = jnp.concatenate([odd, pltpu.roll(even, rows - 1, 2)], axis=1)
+    y_prev = jnp.concatenate([pltpu.roll(odd, 1, 2), even], axis=1)
     result = above + below
-    result = result + pltpu.roll(center, center.shape[1] - 1, 1) + pltpu.roll(center, 1, 1)
-    return result + pltpu.roll(center, center.shape[2] - 1, 2) + pltpu.roll(center, 1, 2)
+    result = result + y_next + y_prev
+    return result + pltpu.roll(center, center.shape[3] - 1, 3) + pltpu.roll(center, 1, 3)
 
 
 def plane_drive(field):
@@ -151,8 +156,8 @@
 
 
 def prep_call(start):
-    count, planes, rows, lanes = start.shape
-    shape = jax.ShapeDtypeStruct((count, planes - 2, rows, lanes), jnp.float32)
+    count, planes = start.shape[:2]
+    shape = jax.ShapeDtypeStruct((count, planes - 2) + start.shape[2:], jnp.float32)
     return pl.pallas_call(
         prep_kernel,
         out_shape=(shape, shape),
@@ -246,32 +251,37 @@
 
 
 def sweep_call(sel, coef, state, rates, start, factor, mobility, halo, depth, first, with_rates):
-    order, goal_planes, rows, lanes = rates.shape[-4:]
+    order, goal_planes = start.shape[0], rates.shape[-4]
+    plane = start.shape[2:]
     picks = sel.shape[0]
     out_planes = goal_planes - 2 * (JACOBI - 1)
-    whole5 = lambda i, sel_ref: (0, 0, 0, 0, 0)
-    whole4 = lambda i, sel_ref: (0, 0, 0, 0)
-    per_node = lambda i, sel_ref: (sel_ref[i], 0, 0, 0, 0)
-    per_out = lambda i, sel_ref: (i, 0, 0, 0, 0)
-    if first:
-        state_spec = pl.BlockSpec(state.shape, whole4)
-    else:
-        state_spec = pl.BlockSpec((1,) + state.shape[1:], per_node)
+
+    def whole(block):
+        return pl.BlockSpec(block.shape, lambda i, sel_ref: (0,) * block.ndim)
+
+    def per_node(block):
+        return pl.BlockSpec(
+            (1,) + block.shape[1:], lambda i, sel_ref: (sel_ref[i],) + (0,) * (block.ndim - 1)
+        )
+
+    def per_out(shape):
+        return pl.BlockSpec((1,) + shape[1:], lambda i, sel_ref: (i,) + (0,) * (len(shape) - 1))
+
     in_specs = [
         pl.BlockSpec(memory_space=pltpu.SMEM),
-        state_spec,
-        pl.BlockSpec(rates.shape, whole4 if first else whole5),
-        pl.BlockSpec(start.shape, whole4),
-        pl.BlockSpec((1,) + factor.shape[1:], per_node),
-        pl.BlockSpec(mobility.shape, whole5) if first else pl.BlockSpec((1,) + mobility.shape[1:], per_node),
+        whole(state) if first else per_node(state),
+        whole(rates),
+        whole(start),
+        per_node(factor),
+        whole(mobility) if first else per_node(mobility),
     ]
-    out_shape = [jax.ShapeDtypeStruct((picks, order, out_planes, rows, lanes), jnp.float32)]
-    out_specs = [pl.BlockSpec((1, order, out_planes, rows, lanes), per_out)]
+    out_dims = [(picks, order, out_planes) + plane]
     if with_rates:
-        out_shape.append(jax.ShapeDtypeStruct((picks, order, out_planes - 2, rows, lanes), jnp.float32))
-        out_specs.append(pl.BlockSpec((1, order, out_planes - 2, rows, lanes), per_out))
-    scratch = [pltpu.VMEM((order, goal_planes, rows, lanes), jnp.float32)]
-    scratch += [pltpu.VMEM((order, goal_planes, rows, lanes), jnp.float32) for _ in range(min(2, JACOBI - 1))]
+        out_dims.append((picks, order, out_planes - 2) + plane)
+    out_shape = [jax.ShapeDtypeStruct(dims, jnp.float32) for dims in out_dims]
+    out_specs = [per_out(dims) for dims in out_dims]
+    scratch = [pltpu.VMEM((order, goal_planes) + plane, jnp.float32)]
+    scratch += [pltpu.VMEM((order, goal_planes) + plane, jnp.float32) for _ in range(min(2, JACOBI - 1))]
     kernel = functools.partial(
         sweep_kernel, halo=halo, depth=depth, first=first, with_rates=with_rates, jacobi=JACOBI
     )
@@ -294,26 +304,28 @@
     total_nodes = lax.axis_size("node") * NODE_DEV
     node_times, table = radau_table(total_nodes)
     times = jnp.asarray(node_times, jnp.float32)
-    taus = times.reshape((total_nodes, 1, 1, 1, 1))
+    taus = times.reshape((total_nodes, 1, 1, 1, 1, 1))
     coef = jnp.asarray(
         np.concatenate([table, node_times[:, None]], axis=1).astype(np.float32)
     )
     mine = lax.axis_index("node") * NODE_DEV
     depth = SWEEPS * JACOBI
     orders = jnp.arange(P_SIZE, dtype=jnp.int32)
-    every = jnp.arange(total_nodes, dtype=jnp.int32)
+    every = jnp.asarray(np.arange(total_nodes, dtype=np.int32))
 
     packed = jnp.stack([grain_ids.astype(jnp.float32), peak_heat])
+    planes, rows, lanes = grain_ids.shape
+    packed = packed.reshape((2, planes, rows // 2, 2, lanes)).transpose((0, 1, 3, 2, 4))
     packed = gather_halo(packed, 1, depth)
     ids_wide = packed[0]
     peak_wide = packed[1]
-    start = (ids_wide[None] == orders[:, None, None, None].astype(jnp.float32)).astype(jnp.float32)
+    start = (ids_wide[None] == orders[:, None, None, None, None].astype(jnp.float32)).astype(jnp.float32)
 
     states = None
     for step_index in range(STEPS):
         last_step = step_index + 1 == STEPS
         moments = (step_index + times) * time_step
-        mobility = heat_mobility(peak_wide[None], moments[:, None, None, None])[:, None]
+        mobility = heat_mobility(peak_wide[None], moments[:, None, None, None, None])[:, None]
         factor = time_step * taus * mobility
         rates, pull = prep_call(start)
         halo = depth
@@ -322,7 +334,10 @@
             last = sweep_index + 1 == SWEEPS
             if last:
                 keep = mine if last_step else total_nodes - 1
-                sel = jnp.reshape(jnp.asarray(keep, jnp.int32), (1,))
+                if last_step:
+                    sel = jnp.reshape(jnp.asarray(keep, jnp.int32), (1,))
+                else:
+                    sel = jnp.asarray(np.array([keep], np.int32))
             else:
                 sel = every
             outs = sweep_call(
@@ -335,7 +350,8 @@
             halo -= JACOBI
         if not last_step:
             start = gather_halo(states[0], 1, depth)
-    return states
+    count, order, planes = states.shape[:3]
+    return states.transpose((0, 1, 2, 4, 3, 5)).reshape((count, order, planes, rows, lanes))
 
 
 def solution(mesh):

time: 133 us -> 128 us (0.962)
  Pallas kernels: 75 us -> 70.8 us
  other arithmetic: 7.3 us -> 5.04 us
    pallas_call x6, Pallas kernels: 68.6 us -> 64.5 us  [sweep_call(): pl.pallas_call(kernel, out_shape=tuple(out_shape), grid_spec=pltpu.Prefet...]
    another operation x3 -> x0, other arithmetic: 2.27 us -> none  [on_device(): packed = jnp.stack([grain_ids.astype(jnp.float32), peak_heat])]
    iota x4 -> x0, local copies, waits for them, and re-layouts: 2.04 us -> none  [on_device(): every = jnp.arange(total_nodes, dtype=jnp.int32)]
  transfers between devices with their start and end apart: 8 -> 8, of which waited for: 2 -> 2; matrix products, arithmetic and copies ran while one was open for 3% -> 2% of each run, Pallas kernels for 0% -> 0%
where the time goes in v4:
time: 128 us; the launch traced here: 127 us
  Pallas kernels  70.8 us (55%)
  starting transfers between devices  41.5 us (32%)
  local copies, waits for them, and re-layouts  6.19 us (5%)
  other arithmetic  5.04 us (4%)
  waiting for transfers between devices  3.07 us (2%)
    pallas_call x6, Pallas kernels, sweep_call(): pl.pallas_call(kernel, out_shape=tuple(out_shape), grid_spec=pltpu.Prefet...  64.5 us
    ppermute x4, starting transfers between devices, gather_halo(): lax.ppermute(lax.slice_in_dim(block, 0, take, axis=dim), axis, down)  33.8 us
    ppermute x4, starting transfers between devices, gather_halo(): lax.ppermute(lax.slice_in_dim(block, size - take, size, axis=dim), axis, up)  7.66 us
    pallas_call x2, Pallas kernels, prep_call(): pl.pallas_call(prep_kernel, out_shape=(shape, shape), in_specs=[pl.BlockS...  6.3 us
    exp x1, other arithmetic, heat_mobility(): return jnp.exp(activation * (1.0 - 1.0 / theta))  3.11 us
    ppermute x4, waiting for transfers between devices, gather_halo(): lax.ppermute(lax.slice_in_dim(block, 0, take, axis=dim), axis, down)  3.02 us
  transfers between devices with their start and end apart: 8, of which 2 were waited for; matrix products, arithmetic and copies ran while one was open for 2% of the time, Pallas kernels for 0%

profile of v4, /device:TPU:24, one launch (start us, length us, event | category | flops | bytes accessed | tf_op | source)
XLA Modules:
  0.0 126.8 jit_solution(6483871262989522543)
XLA Ops:
  0.0 0.8 convert_element_type.14
  0.8 0.8 copy.10
  1.5 1.9 %collective-permute-start.1 = (f32[2,4,2,8,128]{4,3,2,1,0:T(8,128)S(1)}, f32[2,4,2,8,128]{4,3,2,1,0:T(8,128)S(1)}, u32[]{:S(2)}, u32[]{:S(2)}) collective-permute-start(f32[2,4,2,8,128]{4,3,2,1,0:T(8,128)S(1)} %maximum_bitcast_fusion), channel_id=1, source_target_pairs={{0,1},{1,2},{2,3},{3,4},{4,5},{5,6},{6,7},{7,8},{8,9},{9,10},{10,1... | collective-permute-start | bytes 196616 | tf_op jit(solution)/shard_map/ppermute | solution.py:37
  3.5 13.3 %collective-permute-start.2 = (f32[2,4,2,8,128]{4,3,2,1,0:T(8,128)S(1)}, f32[2,4,2,8,128]{4,3,2,1,0:T(8,128)S(1)}, u32[]{:S(2)}, u32[]{:S(2)}) collective-permute-start(f32[2,4,2,8,128]{4,3,2,1,0:T(8,128)S(1)} %maximum_bitcast_fusion), channel_id=1, source_target_pairs={{0,63},{1,0},{2,1},{3,2},{4,3},{5,4},{6,5},{7,6},{8,7},{9,8},{10,9... | collective-permute-start | bytes 196616 | tf_op jit(solution)/shard_map/ppermute | solution.py:38
  16.8 1.9 %collective-permute-start = (f32[2,2,2,8,128]{4,3,2,1,0:T(8,128)S(1)}, f32[2,2,2,8,128]{4,3,2,1,0:T(8,128)S(1)}, u32[]{:S(2)}, u32[]{:S(2)}) collective-permute-start(f32[2,2,2,8,128]{4,3,2,1,0:T(8,128)S(1)} %get-tuple-element.38), channel_id=1, source_target_pairs={{0,2},{1,3},{2,4},{3,5},{4,6},{5,7},{6,8},{7,9},{8,10},{9,11},{10,... | collective-permute-start | bytes 98312 | tf_op jit(solution)/shard_map/ppermute | solution.py:37
  18.7 7.5 %collective-permute-start.3 = (f32[2,2,2,8,128]{4,3,2,1,0:T(8,128)S(1)}, f32[2,2,2,8,128]{4,3,2,1,0:T(8,128)S(1)}, u32[]{:S(2)}, u32[]{:S(2)}) collective-permute-start(f32[2,2,2,8,128]{4,3,2,1,0:T(8,128)S(1)} %get-tuple-element.37), channel_id=1, source_target_pairs={{0,62},{1,63},{2,0},{3,1},{4,2},{5,3},{6,4},{7,5},{8,6},{9,7},{10,... | collective-permute-start | bytes 98312 | tf_op jit(solution)/shard_map/ppermute | solution.py:38
  26.3 0.0 collective-permute-done
  26.3 0.0 collective-permute-done.1
  26.3 0.0 collective-permute-done.2
  26.4 1.5 %collective-permute-done.3 = f32[2,2,2,8,128]{4,3,2,1,0:T(8,128)S(1)} collective-permute-done((f32[2,2,2,8,128]{4,3,2,1,0:T(8,128)S(1)}, f32[2,2,2,8,128]{4,3,2,1,0:T(8,128)S(1)}, u32[]{:S(2)}, u32[]{:S(2)}) %collective-permute-start.3) | collective-permute-done | bytes 32800 | tf_op jit(solution)/shard_map/ppermute | solution.py:38
  27.9 1.1 compare_convert_fusion.start_ref
  29.0 3.2 %shard_map.64 = (f32[8,14,2,8,128]{4,3,2,1,0:T(8,128)}, f32[8,14,2,8,128]{4,3,2,1,0:T(8,128)}) custom-call(f32[8,16,2,8,128]{4,3,2,1,0:T(8,128)} %compare_convert_fusion.start_ref), custom_call_target="tpu_custom_call" | custom-call | tf_op jit(solution)/shard_map/pallas_call | solution.py:161
  32.1 3.1 %multiply_exponential_fusion = (f32[8,1,16,2,8,128]{5,4,3,2,1,0:T(8,128)}, f32[8,1,16,2,8,128]{5,4,3,2,1,0:T(8,128)}, f32[8,1,16,2,8,128]{5,4,3,2,1,0:T(8,128)}, f32[8,1,16,2,8,128]{5,4,3,2,1,0:T(8,128)}) fusion(f32[8]{0:T(128)} %constant.51, f32[16,2,8,128]{3,2,1,0:T(8,128)S(1)} %get-tuple-element.31, f32[8]{0:T(128)} %constant.39, f32[8]{0:T(128)} %constant.44), kind=kLoop, calls=%fused_computation | loop fusion | flops 3145728 | bytes 4325472 | tf_op jit(solution)/shard_map/exp | solution.py:116
  35.3 0.5 call_exported.0.sel_ref
  35.8 13.2 %shard_map.65 = (f32[8,8,12,2,8,128]{5,4,3,2,1,0:T(8,128)}, f32[8,8,10,2,8,128]{5,4,3,2,1,0:T(8,128)}) custom-call(s32[8]{0:T(128)} %call_exported.0.sel_ref, f32[8,9]{1,0:T(8,128)} %constant.35.clone.coef_ref, f32[8,14,2,8,128]{4,3,2,1,0:T(8,128)} %get-tuple-element.17.state_ref, f32[8,14,2,8,128]{4,3,2,1,0:T(8,128)} %get-tuple-element.18.rates_ref, ...), custom_call_target="tpu_custom_call" | custom-call | tf_op jit(solution)/shard_map/pallas_call | solution.py:288
  49.0 15.4 %shard_map.66 = (f32[8,8,8,2,8,128]{5,4,3,2,1,0:T(8,128)}, f32[8,8,6,2,8,128]{5,4,3,2,1,0:T(8,128)}) custom-call(s32[8]{0:T(128)} %call_exported.0.sel_ref, f32[8,9]{1,0:T(8,128)} %constant.35.clone.coef_ref, f32[8,8,12,2,8,128]{5,4,3,2,1,0:T(8,128)} %get-tuple-element.19.state_ref, f32[8,8,10,2,8,128]{5,4,3,2,1,0:T(8,128)} %get-tuple-element.20.rates_ref, ...), custom_call_target="tpu_custom_call" | custom-call | tf_op jit(solution)/shard_map/pallas_call | solution.py:288
  64.4 3.7 %shard_map.67 = f32[1,8,4,2,8,128]{5,4,3,2,1,0:T(8,128)} custom-call(s32[1]{0:T(128)} %constant.36.clone.sel_ref, f32[8,9]{1,0:T(8,128)} %constant.35.clone.coef_ref, f32[8,8,8,2,8,128]{5,4,3,2,1,0:T(8,128)} %get-tuple-element.21.state_ref, f32[8,8,6,2,8,128]{5,4,3,2,1,0:T(8,128)} %get-tuple-element.22.rates_ref, ...), custom_call_target="tpu_custom_call" | custom-call | tf_op jit(solution)/shard_map/pallas_call | solution.py:288
  68.1 1.9 %collective-permute-start.5 = (f32[8,4,2,8,128]{4,3,2,1,0:T(8,128)}, f32[8,4,2,8,128]{4,3,2,1,0:T(8,128)S(1)}, u32[]{:S(2)}, u32[]{:S(2)}) collective-permute-start(f32[8,4,2,8,128]{4,3,2,1,0:T(8,128)} %bitcast.15), channel_id=1, source_target_pairs={{0,1},{1,2},{2,3},{3,4},{4,5},{5,6},{6,7},{7,8},{8,9},{9,10},{10,1... | collective-permute-start | bytes 786440 | tf_op jit(solution)/shard_map/ppermute | solution.py:37
  70.0 1.0 fusion.1
  71.0 1.9 %collective-permute-start.4 = (f32[8,2,2,8,128]{4,3,2,1,0:T(8,128)S(1)}, f32[8,2,2,8,128]{4,3,2,1,0:T(8,128)S(1)}, u32[]{:S(2)}, u32[]{:S(2)}) collective-permute-start(f32[8,2,2,8,128]{4,3,2,1,0:T(8,128)S(1)} %get-tuple-element.30), channel_id=1, source_target_pairs={{0,2},{1,3},{2,4},{3,5},{4,6},{5,7},{6,8},{7,9},{8,10},{9,11},{10,... | collective-permute-start | bytes 393224 | tf_op jit(solution)/shard_map/ppermute | solution.py:37
  72.9 7.3 %collective-permute-start.6 = (f32[8,4,2,8,128]{4,3,2,1,0:T(8,128)}, f32[8,4,2,8,128]{4,3,2,1,0:T(8,128)S(1)}, u32[]{:S(2)}, u32[]{:S(2)}) collective-permute-start(f32[8,4,2,8,128]{4,3,2,1,0:T(8,128)} %bitcast.17), channel_id=1, source_target_pairs={{0,63},{1,0},{2,1},{3,2},{4,3},{5,4},{6,5},{7,6},{8,7},{9,8},{10,9... | collective-permute-start | bytes 786440 | tf_op jit(solution)/shard_map/ppermute | solution.py:38
  80.2 5.7 %collective-permute-start.7 = (f32[8,2,2,8,128]{4,3,2,1,0:T(8,128)S(1)}, f32[8,2,2,8,128]{4,3,2,1,0:T(8,128)S(1)}, u32[]{:S(2)}, u32[]{:S(2)}) collective-permute-start(f32[8,2,2,8,128]{4,3,2,1,0:T(8,128)S(1)} %get-tuple-element.29), channel_id=1, source_target_pairs={{0,62},{1,63},{2,0},{3,1},{4,2},{5,3},{6,4},{7,5},{8,6},{9,7},{10,... | collective-permute-start | bytes 393224 | tf_op jit(solution)/shard_map/ppermute | solution.py:38
  85.9 0.0 collective-permute-done.4
  86.0 1.0 constant_dynamic-update-slice_fusion.7
  87.0 1.5 %collective-permute-done.7 = f32[8,2,2,8,128]{4,3,2,1,0:T(8,128)S(1)} collective-permute-done((f32[8,2,2,8,128]{4,3,2,1,0:T(8,128)S(1)}, f32[8,2,2,8,128]{4,3,2,1,0:T(8,128)S(1)}, u32[]{:S(2)}, u32[]{:S(2)}) %collective-permute-start.7) | collective-permute-done | bytes 131104 | tf_op jit(solution)/shard_map/ppermute | solution.py:38
  88.5 1.0 copy-done
  89.5 3.2 %shard_map.68 = (f32[8,14,2,8,128]{4,3,2,1,0:T(8,128)}, f32[8,14,2,8,128]{4,3,2,1,0:T(8,128)}) custom-call(f32[8,16,2,8,128]{4,3,2,1,0:T(8,128)} %copy-done), custom_call_target="tpu_custom_call" | custom-call | tf_op jit(solution)/shard_map/pallas_call | solution.py:161
  92.7 13.2 %shard_map.69 = (f32[8,8,12,2,8,128]{5,4,3,2,1,0:T(8,128)}, f32[8,8,10,2,8,128]{5,4,3,2,1,0:T(8,128)}) custom-call(s32[8]{0:T(128)} %call_exported.0.sel_ref, f32[8,9]{1,0:T(8,128)} %constant.35.clone.coef_ref, f32[8,14,2,8,128]{4,3,2,1,0:T(8,128)} %get-tuple-element.23.state_ref, f32[8,14,2,8,128]{4,3,2,1,0:T(8,128)} %get-tuple-element.24.rates_ref, ...), custom_call_target="tpu_custom_call" | custom-call | tf_op jit(solution)/shard_map/pallas_call | solution.py:288
  105.9 15.4 %shard_map.70 = (f32[8,8,8,2,8,128]{5,4,3,2,1,0:T(8,128)}, f32[8,8,6,2,8,128]{5,4,3,2,1,0:T(8,128)}) custom-call(s32[8]{0:T(128)} %call_exported.0.sel_ref, f32[8,9]{1,0:T(8,128)} %constant.35.clone.coef_ref, f32[8,8,12,2,8,128]{5,4,3,2,1,0:T(8,128)} %get-tuple-element.25.state_ref, f32[8,8,10,2,8,128]{5,4,3,2,1,0:T(8,128)} %get-tuple-element.26.rates_ref, ...), custom_call_target="tpu_custom_call" | custom-call | tf_op jit(solution)/shard_map/pallas_call | solution.py:288
  121.2 3.7 %shard_map.71 = f32[1,8,4,2,8,128]{5,4,3,2,1,0:T(8,128)} custom-call(s32[1]{0:T(128)} %bitcast.sel_ref, f32[8,9]{1,0:T(8,128)} %constant.35.clone.coef_ref, f32[8,8,8,2,8,128]{5,4,3,2,1,0:T(8,128)} %get-tuple-element.27.state_ref, f32[8,8,6,2,8,128]{5,4,3,2,1,0:T(8,128)} %get-tuple-element.28.rates_ref, f32[8,16,2,8,128]{4,3,2,1,0:T(8,128)} %copy-done, ...), custom_call_target="tpu_custom_call" | custom-call | tf_op jit(solution)/shard_map/pallas_call | solution.py:288
  124.9 1.1 copy.11
  126.0 0.8 copy.12
  (17 shorter events, 0.1 us)
Async XLA Ops:
  1.5 24.8 %collective-permute-start.1 = (f32[2,4,2,8,128]{4,3,2,1,0:T(8,128)S(1)}, f32[2,4,2,8,128]{4,3,2,1,0:T(8,128)S(1)}, u32[]{:S(2)}, u32[]{:S(2)}) collective-permute-start(f32[2,4,2,8,128]{4,3,2,1,0:T(8,128)S(1)} %maximum_bitcast_fusion), channel_id=1, source_target_pairs={{0,1},{1,2},{2,3},{3,4},{4,5},{5,6},{6,7},{7,8},{8,9},{9,10},{10,1... | collective-permute-start | bytes 196616 | tf_op jit(solution)/shard_map/ppermute | solution.py:37
  3.5 22.9 %collective-permute-start.2 = (f32[2,4,2,8,128]{4,3,2,1,0:T(8,128)S(1)}, f32[2,4,2,8,128]{4,3,2,1,0:T(8,128)S(1)}, u32[]{:S(2)}, u32[]{:S(2)}) collective-permute-start(f32[2,4,2,8,128]{4,3,2,1,0:T(8,128)S(1)} %maximum_bitcast_fusion), channel_id=1, source_target_pairs={{0,63},{1,0},{2,1},{3,2},{4,3},{5,4},{6,5},{7,6},{8,7},{9,8},{10,9... | collective-permute-start | bytes 196616 | tf_op jit(solution)/shard_map/ppermute | solution.py:38
  16.8 9.5 %collective-permute-start = (f32[2,2,2,8,128]{4,3,2,1,0:T(8,128)S(1)}, f32[2,2,2,8,128]{4,3,2,1,0:T(8,128)S(1)}, u32[]{:S(2)}, u32[]{:S(2)}) collective-permute-start(f32[2,2,2,8,128]{4,3,2,1,0:T(8,128)S(1)} %get-tuple-element.38), channel_id=1, source_target_pairs={{0,2},{1,3},{2,4},{3,5},{4,6},{5,7},{6,8},{7,9},{8,10},{9,11},{10,... | collective-permute-start | bytes 98312 | tf_op jit(solution)/shard_map/ppermute | solution.py:37
  18.7 9.1 %collective-permute-start.3 = (f32[2,2,2,8,128]{4,3,2,1,0:T(8,128)S(1)}, f32[2,2,2,8,128]{4,3,2,1,0:T(8,128)S(1)}, u32[]{:S(2)}, u32[]{:S(2)}) collective-permute-start(f32[2,2,2,8,128]{4,3,2,1,0:T(8,128)S(1)} %get-tuple-element.37), channel_id=1, source_target_pairs={{0,62},{1,63},{2,0},{3,1},{4,2},{5,3},{6,4},{7,5},{8,6},{9,7},{10,... | collective-permute-start | bytes 98312 | tf_op jit(solution)/shard_map/ppermute | solution.py:38
  68.1 17.9 %collective-permute-start.5 = (f32[8,4,2,8,128]{4,3,2,1,0:T(8,128)}, f32[8,4,2,8,128]{4,3,2,1,0:T(8,128)S(1)}, u32[]{:S(2)}, u32[]{:S(2)}) collective-permute-start(f32[8,4,2,8,128]{4,3,2,1,0:T(8,128)} %bitcast.15), channel_id=1, source_target_pairs={{0,1},{1,2},{2,3},{3,4},{4,5},{5,6},{6,7},{7,8},{8,9},{9,10},{10,1... | collective-permute-start | bytes 786440 | tf_op jit(solution)/shard_map/ppermute | solution.py:37
  71.0 14.9 %collective-permute-start.4 = (f32[8,2,2,8,128]{4,3,2,1,0:T(8,128)S(1)}, f32[8,2,2,8,128]{4,3,2,1,0:T(8,128)S(1)}, u32[]{:S(2)}, u32[]{:S(2)}) collective-permute-start(f32[8,2,2,8,128]{4,3,2,1,0:T(8,128)S(1)} %get-tuple-element.30), channel_id=1, source_target_pairs={{0,2},{1,3},{2,4},{3,5},{4,6},{5,7},{6,8},{7,9},{8,10},{9,11},{10,... | collective-permute-start | bytes 393224 | tf_op jit(solution)/shard_map/ppermute | solution.py:37
  72.9 14.0 %collective-permute-start.6 = (f32[8,4,2,8,128]{4,3,2,1,0:T(8,128)}, f32[8,4,2,8,128]{4,3,2,1,0:T(8,128)S(1)}, u32[]{:S(2)}, u32[]{:S(2)}) collective-permute-start(f32[8,4,2,8,128]{4,3,2,1,0:T(8,128)} %bitcast.17), channel_id=1, source_target_pairs={{0,63},{1,0},{2,1},{3,2},{4,3},{5,4},{6,5},{7,6},{8,7},{9,8},{10,9... | collective-permute-start | bytes 786440 | tf_op jit(solution)/shard_map/ppermute | solution.py:38
  80.2 8.4 %collective-permute-start.7 = (f32[8,2,2,8,128]{4,3,2,1,0:T(8,128)S(1)}, f32[8,2,2,8,128]{4,3,2,1,0:T(8,128)S(1)}, u32[]{:S(2)}, u32[]{:S(2)}) collective-permute-start(f32[8,2,2,8,128]{4,3,2,1,0:T(8,128)S(1)} %get-tuple-element.29), channel_id=1, source_target_pairs={{0,62},{1,63},{2,0},{3,1},{4,2},{5,3},{6,4},{7,5},{8,6},{9,7},{10,... | collective-permute-start | bytes 393224 | tf_op jit(solution)/shard_map/ppermute | solution.py:38
  88.5 1.0 copy-start

commit v5 on v4

--- a/solution.py
+++ b/solution.py
@@ -177,13 +177,9 @@
         out_rates_ref = None
     node = sel_ref[pl.program_id(0)]
     count = rates_ref.shape[0]
-    if not first:
-        dt_tau = time_step * coef_ref[node, count]
-        weights = [coef_ref[node, j] for j in range(count)]
     if first:
         count = mob_ref.shape[0]
-        weights = [coef_ref[node, j] for j in range(count)]
-        dt_tau = time_step * coef_ref[node, count]
+    weights = [coef_ref[node, j] for j in range(count)]
     goal_planes = goal_sc.shape[1]
     off_goal = depth - (halo - 1)
 
@@ -193,13 +189,12 @@
             mix = -mob_ref[0, :, z + off_goal] * weights[0]
             for j in range(1, count):
                 mix = mix + -mob_ref[j, :, z + off_goal] * weights[j]
-            own = -mob_ref[node, :, z + off_goal] * bracket
-            goal_sc[:, z] = start_ref[:, z + off_goal] + time_step * (mix * bracket) - dt_tau * own
+            goal_sc[:, z] = start_ref[:, z + off_goal] + mix * bracket
         else:
             acc = rates_ref[0, :, z] * weights[0]
             for j in range(1, count):
                 acc = acc + rates_ref[j, :, z] * weights[j]
-            goal_sc[:, z] = start_ref[:, z + off_goal] + time_step * acc - dt_tau * rates_ref[node, :, z]
+            goal_sc[:, z] = start_ref[:, z + off_goal] + acc
         return carry
 
     lax.fori_loop(0, goal_planes, goal_body, 0, unroll=True)
@@ -306,7 +301,7 @@
     times = jnp.asarray(node_times, jnp.float32)
     taus = times.reshape((total_nodes, 1, 1, 1, 1, 1))
     coef = jnp.asarray(
-        np.concatenate([table, node_times[:, None]], axis=1).astype(np.float32)
+        (time_step * table - time_step * np.diag(node_times)).astype(np.float32)
     )
     mine = lax.axis_index("node") * NODE_DEV
     depth = SWEEPS * JACOBI

time: 128 us -> 126 us (0.984)
  Pallas kernels: 70.8 us -> 67.9 us
    pallas_call x6, Pallas kernels: 64.5 us -> 61.6 us  [sweep_call(): pl.pallas_call(kernel, out_shape=tuple(out_shape), grid_spec=pltpu.Prefet...]
where the time goes in v5:
time: 126 us; the launch traced here: 124 us
  Pallas kernels  67.9 us (54%)
  starting transfers between devices  41.5 us (33%)
  local copies, waits for them, and re-layouts  6.19 us (5%)
  other arithmetic  5.04 us (4%)
  waiting for transfers between devices  3.07 us (2%)
    pallas_call x6, Pallas kernels, sweep_call(): pl.pallas_call(kernel, out_shape=tuple(out_shape), grid_spec=pltpu.Prefet...  61.6 us
    ppermute x4, starting transfers between devices, gather_halo(): lax.ppermute(lax.slice_in_dim(block, 0, take, axis=dim), axis, down)  33.8 us
    ppermute x4, starting transfers between devices, gather_halo(): lax.ppermute(lax.slice_in_dim(block, size - take, size, axis=dim), axis, up)  7.66 us
    pallas_call x2, Pallas kernels, prep_call(): pl.pallas_call(prep_kernel, out_shape=(shape, shape), in_specs=[pl.BlockS...  6.3 us
    exp x1, other arithmetic, heat_mobility(): return jnp.exp(activation * (1.0 - 1.0 / theta))  3.11 us
    ppermute x4, waiting for transfers between devices, gather_halo(): lax.ppermute(lax.slice_in_dim(block, 0, take, axis=dim), axis, down)  3.02 us
  transfers between devices with their start and end apart: 8, of which 2 were waited for; matrix products, arithmetic and copies ran while one was open for 2% of the time, Pallas kernels for 0%

profile of v5, /device:TPU:24, one launch (start us, length us, event | category | flops | bytes accessed | tf_op | source)
XLA Modules:
  0.0 123.9 jit_solution(6792392756649951918)
XLA Ops:
  0.0 0.8 convert_element_type.14
  0.8 0.8 copy.10
  1.5 1.9 %collective-permute-start.1 = (f32[2,4,2,8,128]{4,3,2,1,0:T(8,128)S(1)}, f32[2,4,2,8,128]{4,3,2,1,0:T(8,128)S(1)}, u32[]{:S(2)}, u32[]{:S(2)}) collective-permute-start(f32[2,4,2,8,128]{4,3,2,1,0:T(8,128)S(1)} %maximum_bitcast_fusion), channel_id=1, source_target_pairs={{0,1},{1,2},{2,3},{3,4},{4,5},{5,6},{6,7},{7,8},{8,9},{9,10},{10,1... | collective-permute-start | bytes 196616 | tf_op jit(solution)/shard_map/ppermute | solution.py:37
  3.5 13.3 %collective-permute-start.2 = (f32[2,4,2,8,128]{4,3,2,1,0:T(8,128)S(1)}, f32[2,4,2,8,128]{4,3,2,1,0:T(8,128)S(1)}, u32[]{:S(2)}, u32[]{:S(2)}) collective-permute-start(f32[2,4,2,8,128]{4,3,2,1,0:T(8,128)S(1)} %maximum_bitcast_fusion), channel_id=1, source_target_pairs={{0,63},{1,0},{2,1},{3,2},{4,3},{5,4},{6,5},{7,6},{8,7},{9,8},{10,9... | collective-permute-start | bytes 196616 | tf_op jit(solution)/shard_map/ppermute | solution.py:38
  16.8 1.9 %collective-permute-start = (f32[2,2,2,8,128]{4,3,2,1,0:T(8,128)S(1)}, f32[2,2,2,8,128]{4,3,2,1,0:T(8,128)S(1)}, u32[]{:S(2)}, u32[]{:S(2)}) collective-permute-start(f32[2,2,2,8,128]{4,3,2,1,0:T(8,128)S(1)} %get-tuple-element.38), channel_id=1, source_target_pairs={{0,2},{1,3},{2,4},{3,5},{4,6},{5,7},{6,8},{7,9},{8,10},{9,11},{10,... | collective-permute-start | bytes 98312 | tf_op jit(solution)/shard_map/ppermute | solution.py:37
  18.7 7.5 %collective-permute-start.3 = (f32[2,2,2,8,128]{4,3,2,1,0:T(8,128)S(1)}, f32[2,2,2,8,128]{4,3,2,1,0:T(8,128)S(1)}, u32[]{:S(2)}, u32[]{:S(2)}) collective-permute-start(f32[2,2,2,8,128]{4,3,2,1,0:T(8,128)S(1)} %get-tuple-element.37), channel_id=1, source_target_pairs={{0,62},{1,63},{2,0},{3,1},{4,2},{5,3},{6,4},{7,5},{8,6},{9,7},{10,... | collective-permute-start | bytes 98312 | tf_op jit(solution)/shard_map/ppermute | solution.py:38
  26.3 0.0 collective-permute-done
  26.3 0.0 collective-permute-done.1
  26.4 1.5 %collective-permute-done.3 = f32[2,2,2,8,128]{4,3,2,1,0:T(8,128)S(1)} collective-permute-done((f32[2,2,2,8,128]{4,3,2,1,0:T(8,128)S(1)}, f32[2,2,2,8,128]{4,3,2,1,0:T(8,128)S(1)}, u32[]{:S(2)}, u32[]{:S(2)}) %collective-permute-start.3) | collective-permute-done | bytes 32800 | tf_op jit(solution)/shard_map/ppermute | solution.py:38
  27.9 1.1 compare_convert_fusion.start_ref
  29.0 3.2 %shard_map.64 = (f32[8,14,2,8,128]{4,3,2,1,0:T(8,128)}, f32[8,14,2,8,128]{4,3,2,1,0:T(8,128)}) custom-call(f32[8,16,2,8,128]{4,3,2,1,0:T(8,128)} %compare_convert_fusion.start_ref), custom_call_target="tpu_custom_call" | custom-call | tf_op jit(solution)/shard_map/pallas_call | solution.py:161
  32.1 3.1 %multiply_exponential_fusion = (f32[8,1,16,2,8,128]{5,4,3,2,1,0:T(8,128)}, f32[8,1,16,2,8,128]{5,4,3,2,1,0:T(8,128)}, f32[8,1,16,2,8,128]{5,4,3,2,1,0:T(8,128)}, f32[8,1,16,2,8,128]{5,4,3,2,1,0:T(8,128)}) fusion(f32[8]{0:T(128)} %constant.51, f32[16,2,8,128]{3,2,1,0:T(8,128)S(1)} %get-tuple-element.31, f32[8]{0:T(128)} %constant.39, f32[8]{0:T(128)} %constant.44), kind=kLoop, calls=%fused_computation | loop fusion | flops 3145728 | bytes 4325472 | tf_op jit(solution)/shard_map/exp | solution.py:116
  35.3 0.5 call_exported.0.sel_ref
  35.8 12.2 %shard_map.65 = (f32[8,8,12,2,8,128]{5,4,3,2,1,0:T(8,128)}, f32[8,8,10,2,8,128]{5,4,3,2,1,0:T(8,128)}) custom-call(s32[8]{0:T(128)} %call_exported.0.sel_ref, f32[8,8]{1,0:T(8,128)} %constant.35.clone.coef_ref, f32[8,14,2,8,128]{4,3,2,1,0:T(8,128)} %get-tuple-element.17.state_ref, f32[8,14,2,8,128]{4,3,2,1,0:T(8,128)} %get-tuple-element.18.rates_ref, ...), custom_call_target="tpu_custom_call" | custom-call | tf_op jit(solution)/shard_map/pallas_call | solution.py:283
  48.0 15.0 %shard_map.66 = (f32[8,8,8,2,8,128]{5,4,3,2,1,0:T(8,128)}, f32[8,8,6,2,8,128]{5,4,3,2,1,0:T(8,128)}) custom-call(s32[8]{0:T(128)} %call_exported.0.sel_ref, f32[8,8]{1,0:T(8,128)} %constant.35.clone.coef_ref, f32[8,8,12,2,8,128]{5,4,3,2,1,0:T(8,128)} %get-tuple-element.19.state_ref, f32[8,8,10,2,8,128]{5,4,3,2,1,0:T(8,128)} %get-tuple-element.20.rates_ref, ...), custom_call_target="tpu_custom_call" | custom-call | tf_op jit(solution)/shard_map/pallas_call | solution.py:283
  63.0 3.6 %shard_map.67 = f32[1,8,4,2,8,128]{5,4,3,2,1,0:T(8,128)} custom-call(s32[1]{0:T(128)} %constant.36.clone.sel_ref, f32[8,8]{1,0:T(8,128)} %constant.35.clone.coef_ref, f32[8,8,8,2,8,128]{5,4,3,2,1,0:T(8,128)} %get-tuple-element.21.state_ref, f32[8,8,6,2,8,128]{5,4,3,2,1,0:T(8,128)} %get-tuple-element.22.rates_ref, ...), custom_call_target="tpu_custom_call" | custom-call | tf_op jit(solution)/shard_map/pallas_call | solution.py:283
  66.6 1.9 %collective-permute-start.5 = (f32[8,4,2,8,128]{4,3,2,1,0:T(8,128)}, f32[8,4,2,8,128]{4,3,2,1,0:T(8,128)S(1)}, u32[]{:S(2)}, u32[]{:S(2)}) collective-permute-start(f32[8,4,2,8,128]{4,3,2,1,0:T(8,128)} %bitcast.15), channel_id=1, source_target_pairs={{0,1},{1,2},{2,3},{3,4},{4,5},{5,6},{6,7},{7,8},{8,9},{9,10},{10,1... | collective-permute-start | bytes 786440 | tf_op jit(solution)/shard_map/ppermute | solution.py:37
  68.5 1.0 fusion.1
  69.5 1.9 %collective-permute-start.4 = (f32[8,2,2,8,128]{4,3,2,1,0:T(8,128)S(1)}, f32[8,2,2,8,128]{4,3,2,1,0:T(8,128)S(1)}, u32[]{:S(2)}, u32[]{:S(2)}) collective-permute-start(f32[8,2,2,8,128]{4,3,2,1,0:T(8,128)S(1)} %get-tuple-element.30), channel_id=1, source_target_pairs={{0,2},{1,3},{2,4},{3,5},{4,6},{5,7},{6,8},{7,9},{8,10},{9,11},{10,... | collective-permute-start | bytes 393224 | tf_op jit(solution)/shard_map/ppermute | solution.py:37
  71.5 7.3 %collective-permute-start.6 = (f32[8,4,2,8,128]{4,3,2,1,0:T(8,128)}, f32[8,4,2,8,128]{4,3,2,1,0:T(8,128)S(1)}, u32[]{:S(2)}, u32[]{:S(2)}) collective-permute-start(f32[8,4,2,8,128]{4,3,2,1,0:T(8,128)} %bitcast.17), channel_id=1, source_target_pairs={{0,63},{1,0},{2,1},{3,2},{4,3},{5,4},{6,5},{7,6},{8,7},{9,8},{10,9... | collective-permute-start | bytes 786440 | tf_op jit(solution)/shard_map/ppermute | solution.py:38
  78.7 5.7 %collective-permute-start.7 = (f32[8,2,2,8,128]{4,3,2,1,0:T(8,128)S(1)}, f32[8,2,2,8,128]{4,3,2,1,0:T(8,128)S(1)}, u32[]{:S(2)}, u32[]{:S(2)}) collective-permute-start(f32[8,2,2,8,128]{4,3,2,1,0:T(8,128)S(1)} %get-tuple-element.29), channel_id=1, source_target_pairs={{0,62},{1,63},{2,0},{3,1},{4,2},{5,3},{6,4},{7,5},{8,6},{9,7},{10,... | collective-permute-start | bytes 393224 | tf_op jit(solution)/shard_map/ppermute | solution.py:38
  84.5 0.0 collective-permute-done.5
  84.5 1.0 constant_dynamic-update-slice_fusion.7
  85.5 0.0 collective-permute-done.6
  85.5 1.5 %collective-permute-done.7 = f32[8,2,2,8,128]{4,3,2,1,0:T(8,128)S(1)} collective-permute-done((f32[8,2,2,8,128]{4,3,2,1,0:T(8,128)S(1)}, f32[8,2,2,8,128]{4,3,2,1,0:T(8,128)S(1)}, u32[]{:S(2)}, u32[]{:S(2)}) %collective-permute-start.7) | collective-permute-done | bytes 131104 | tf_op jit(solution)/shard_map/ppermute | solution.py:38
  87.1 1.0 copy-done
  88.1 3.2 %shard_map.68 = (f32[8,14,2,8,128]{4,3,2,1,0:T(8,128)}, f32[8,14,2,8,128]{4,3,2,1,0:T(8,128)}) custom-call(f32[8,16,2,8,128]{4,3,2,1,0:T(8,128)} %copy-done), custom_call_target="tpu_custom_call" | custom-call | tf_op jit(solution)/shard_map/pallas_call | solution.py:161
  91.2 12.2 %shard_map.69 = (f32[8,8,12,2,8,128]{5,4,3,2,1,0:T(8,128)}, f32[8,8,10,2,8,128]{5,4,3,2,1,0:T(8,128)}) custom-call(s32[8]{0:T(128)} %call_exported.0.sel_ref, f32[8,8]{1,0:T(8,128)} %constant.35.clone.coef_ref, f32[8,14,2,8,128]{4,3,2,1,0:T(8,128)} %get-tuple-element.23.state_ref, f32[8,14,2,8,128]{4,3,2,1,0:T(8,128)} %get-tuple-element.24.rates_ref, ...), custom_call_target="tpu_custom_call" | custom-call | tf_op jit(solution)/shard_map/pallas_call | solution.py:283
  103.4 15.0 %shard_map.70 = (f32[8,8,8,2,8,128]{5,4,3,2,1,0:T(8,128)}, f32[8,8,6,2,8,128]{5,4,3,2,1,0:T(8,128)}) custom-call(s32[8]{0:T(128)} %call_exported.0.sel_ref, f32[8,8]{1,0:T(8,128)} %constant.35.clone.coef_ref, f32[8,8,12,2,8,128]{5,4,3,2,1,0:T(8,128)} %get-tuple-element.25.state_ref, f32[8,8,10,2,8,128]{5,4,3,2,1,0:T(8,128)} %get-tuple-element.26.rates_ref, ...), custom_call_target="tpu_custom_call" | custom-call | tf_op jit(solution)/shard_map/pallas_call | solution.py:283
  118.4 3.6 %shard_map.71 = f32[1,8,4,2,8,128]{5,4,3,2,1,0:T(8,128)} custom-call(s32[1]{0:T(128)} %bitcast.sel_ref, f32[8,8]{1,0:T(8,128)} %constant.35.clone.coef_ref, f32[8,8,8,2,8,128]{5,4,3,2,1,0:T(8,128)} %get-tuple-element.27.state_ref, f32[8,8,6,2,8,128]{5,4,3,2,1,0:T(8,128)} %get-tuple-element.28.rates_ref, f32[8,16,2,8,128]{4,3,2,1,0:T(8,128)} %copy-done, ...), custom_call_target="tpu_custom_call" | custom-call | tf_op jit(solution)/shard_map/pallas_call | solution.py:283
  122.1 1.1 copy.11
  123.2 0.8 copy.12
  (17 shorter events, 0.1 us)
Async XLA Ops:
  1.5 24.8 %collective-permute-start.1 = (f32[2,4,2,8,128]{4,3,2,1,0:T(8,128)S(1)}, f32[2,4,2,8,128]{4,3,2,1,0:T(8,128)S(1)}, u32[]{:S(2)}, u32[]{:S(2)}) collective-permute-start(f32[2,4,2,8,128]{4,3,2,1,0:T(8,128)S(1)} %maximum_bitcast_fusion), channel_id=1, source_target_pairs={{0,1},{1,2},{2,3},{3,4},{4,5},{5,6},{6,7},{7,8},{8,9},{9,10},{10,1... | collective-permute-start | bytes 196616 | tf_op jit(solution)/shard_map/ppermute | solution.py:37
  3.5 22.9 %collective-permute-start.2 = (f32[2,4,2,8,128]{4,3,2,1,0:T(8,128)S(1)}, f32[2,4,2,8,128]{4,3,2,1,0:T(8,128)S(1)}, u32[]{:S(2)}, u32[]{:S(2)}) collective-permute-start(f32[2,4,2,8,128]{4,3,2,1,0:T(8,128)S(1)} %maximum_bitcast_fusion), channel_id=1, source_target_pairs={{0,63},{1,0},{2,1},{3,2},{4,3},{5,4},{6,5},{7,6},{8,7},{9,8},{10,9... | collective-permute-start | bytes 196616 | tf_op jit(solution)/shard_map/ppermute | solution.py:38
  16.8 9.5 %collective-permute-start = (f32[2,2,2,8,128]{4,3,2,1,0:T(8,128)S(1)}, f32[2,2,2,8,128]{4,3,2,1,0:T(8,128)S(1)}, u32[]{:S(2)}, u32[]{:S(2)}) collective-permute-start(f32[2,2,2,8,128]{4,3,2,1,0:T(8,128)S(1)} %get-tuple-element.38), channel_id=1, source_target_pairs={{0,2},{1,3},{2,4},{3,5},{4,6},{5,7},{6,8},{7,9},{8,10},{9,11},{10,... | collective-permute-start | bytes 98312 | tf_op jit(solution)/shard_map/ppermute | solution.py:37
  18.7 9.1 %collective-permute-start.3 = (f32[2,2,2,8,128]{4,3,2,1,0:T(8,128)S(1)}, f32[2,2,2,8,128]{4,3,2,1,0:T(8,128)S(1)}, u32[]{:S(2)}, u32[]{:S(2)}) collective-permute-start(f32[2,2,2,8,128]{4,3,2,1,0:T(8,128)S(1)} %get-tuple-element.37), channel_id=1, source_target_pairs={{0,62},{1,63},{2,0},{3,1},{4,2},{5,3},{6,4},{7,5},{8,6},{9,7},{10,... | collective-permute-start | bytes 98312 | tf_op jit(solution)/shard_map/ppermute | solution.py:38
  66.6 17.9 %collective-permute-start.5 = (f32[8,4,2,8,128]{4,3,2,1,0:T(8,128)}, f32[8,4,2,8,128]{4,3,2,1,0:T(8,128)S(1)}, u32[]{:S(2)}, u32[]{:S(2)}) collective-permute-start(f32[8,4,2,8,128]{4,3,2,1,0:T(8,128)} %bitcast.15), channel_id=1, source_target_pairs={{0,1},{1,2},{2,3},{3,4},{4,5},{5,6},{6,7},{7,8},{8,9},{9,10},{10,1... | collective-permute-start | bytes 786440 | tf_op jit(solution)/shard_map/ppermute | solution.py:37
  69.5 14.9 %collective-permute-start.4 = (f32[8,2,2,8,128]{4,3,2,1,0:T(8,128)S(1)}, f32[8,2,2,8,128]{4,3,2,1,0:T(8,128)S(1)}, u32[]{:S(2)}, u32[]{:S(2)}) collective-permute-start(f32[8,2,2,8,128]{4,3,2,1,0:T(8,128)S(1)} %get-tuple-element.30), channel_id=1, source_target_pairs={{0,2},{1,3},{2,4},{3,5},{4,6},{5,7},{6,8},{7,9},{8,10},{9,11},{10,... | collective-permute-start | bytes 393224 | tf_op jit(solution)/shard_map/ppermute | solution.py:37
  71.5 14.0 %collective-permute-start.6 = (f32[8,4,2,8,128]{4,3,2,1,0:T(8,128)}, f32[8,4,2,8,128]{4,3,2,1,0:T(8,128)S(1)}, u32[]{:S(2)}, u32[]{:S(2)}) collective-permute-start(f32[8,4,2,8,128]{4,3,2,1,0:T(8,128)} %bitcast.17), channel_id=1, source_target_pairs={{0,63},{1,0},{2,1},{3,2},{4,3},{5,4},{6,5},{7,6},{8,7},{9,8},{10,9... | collective-permute-start | bytes 786440 | tf_op jit(solution)/shard_map/ppermute | solution.py:38
  78.7 8.4 %collective-permute-start.7 = (f32[8,2,2,8,128]{4,3,2,1,0:T(8,128)S(1)}, f32[8,2,2,8,128]{4,3,2,1,0:T(8,128)S(1)}, u32[]{:S(2)}, u32[]{:S(2)}) collective-permute-start(f32[8,2,2,8,128]{4,3,2,1,0:T(8,128)S(1)} %get-tuple-element.29), channel_id=1, source_target_pairs={{0,62},{1,63},{2,0},{3,1},{4,2},{5,3},{6,4},{7,5},{8,6},{9,7},{10,... | collective-permute-start | bytes 393224 | tf_op jit(solution)/shard_map/ppermute | solution.py:38
  87.1 1.0 copy-start
